TPU v7x, 128 devices: a whole 4x4x4 slice. The times are simulated.
128 devices in a mesh: seq: 64 (over z, x, y), tp: 2 (over core).
Axes of the slice: x: 4, y: 4, z: 4, core: 2. Of those that a mesh axis runs over, the one named last changes fastest.
Arguments:
- layer_input: bfloat16 [16384, 2048], P('seq'), may hold values from -1.5 to 1.5
- query: bfloat16 [16384, 2048], P('seq', 'tp'), may hold values from -6 to 6
- suffix_kv: bfloat16 [2, 16384, 2048], P(None, 'seq', 'tp'), may hold values from -6 to 6
- prefix_kv: bfloat16 [2, 2048, 2048], P(None, 'seq', 'tp'), may hold values from -6 to 6
- node_len: int32 [64], replicated, may hold values from 8 to 32, as said below
- path: int32 [64, 3], P('seq'), may hold values from 0 to 63, as said below
- out_weight: bfloat16 [2048, 2048], P('tp'), may hold values from -0.125 to 0.125
- norm_gain: float32 [2048], replicated, may hold values from 0.1 to 1.9
- expert_ids: int32 [16384, 8], P('seq'), may hold values from 0 to 63, all different within a row; in each aligned block of 256 rows (0 to 255, 256 to 511, ...) at most 40 rows name the same one
- gates: float32 [16384, 8], P('seq'), may hold values from 0.1 to 0.4
- w_gate: bfloat16 [64, 2048, 1024], P('seq', None, 'tp'), may hold values from -0.125 to 0.125
- w_up: bfloat16 [64, 2048, 1024], P('seq', None, 'tp'), may hold values from -0.125 to 0.125
- w_down: bfloat16 [64, 1024, 2048], P('seq', 'tp'), may hold values from -0.1875 to 0.1875
Outputs:
- layer_out: bfloat16 [16384, 2048], P('seq', 'tp')
Inputs may be any that keep to these rules, and one draw needn't show every extreme that they name: `path`: row r names three different nodes. Nodes are of three levels: roots, middle nodes and leaves; a middle node always comes with the same root, a leaf always with the same middle node, and every node is named by some request. `node_len`: some node holds exactly 32 tokens. `expert_ids`: within the 256 rows of one request no expert is named more than 40 times, a bound that some block reaches.
All inputs are finite; a program needn't handle non-finite values.
Results may differ from a plain program's by a relative error of at most 0.019.
Values may be sent and summed in bfloat16 or wider, within the bound.
No kernel may reach another device: no remote copies, remote signals or barrier semaphores. Data moves between devices by JAX's collectives and lax.ppermute only.
A program may use at most 128 MiB of HBM per device.

v0:
```python
import math

import jax
import jax.numpy as jnp
from jax import lax
from jax.sharding import PartitionSpec as P

D = 2048
HD = 128
TOPK = 8
SLOT = 32


def slot_plan(ids, experts, cap):
    flat = ids.reshape(-1)
    onehot = (flat[:, None] == jnp.arange(experts, dtype=jnp.int32)[None, :]).astype(jnp.int32)
    rank = jnp.sum(jnp.cumsum(onehot, axis=0) * onehot, axis=1) - 1
    return flat * cap + rank


def local(
    layer_input,
    query,
    suffix_kv,
    prefix_kv,
    node_len,
    path,
    out_weight,
    norm_gain,
    expert_ids,
    gates,
    w_gate,
    w_up,
    w_down,
):
    rows = query.shape[0]
    heads_here = query.shape[1] // HD
    scale = 1.0 / math.sqrt(HD)
    queries = query.reshape(rows, heads_here, HD)
    own_keys = suffix_kv[0].reshape(rows, heads_here, HD)
    own_values = suffix_kv[1].reshape(rows, heads_here, HD).astype(jnp.float32)
    scores = (
        jnp.einsum("qhd,khd->hqk", queries, own_keys, preferred_element_type=jnp.float32) * scale
    )
    top = jnp.max(scores, axis=2)
    probs = jnp.exp(scores - top[:, :, None])
    total = jnp.sum(probs, axis=2)
    accum = jnp.einsum("hqk,khd->hqd", probs, own_values)
    my_nodes = path[0]
    node_ids = jnp.arange(node_len.shape[0], dtype=jnp.int32)
    piece = lax.all_gather(prefix_kv, "seq", axis=1, tiled=True)
    start = jnp.int32(0)
    count = piece.shape[1]

    def absorb(state):
        best, mass, sums = state
        index = jnp.arange(count, dtype=jnp.int32)
        node = index // SLOT
        offset = index % SLOT
        match = node[:, None] == node_ids[None, :]
        lengths = jnp.sum(jnp.where(match, node_len[None, :], 0), axis=1)
        live = (offset < lengths) & jnp.any(node[:, None] == my_nodes[None, :], axis=1)
        piece_keys = piece[0].reshape(count, heads_here, HD)
        piece_values = piece[1].reshape(count, heads_here, HD).astype(jnp.float32)
        block = (
            jnp.einsum("qhd,khd->hqk", queries, piece_keys, preferred_element_type=jnp.float32)
            * scale
        )
        block = jnp.where(live[None, None, :], block, -jnp.inf)
        new_best = jnp.maximum(best, jnp.max(block, axis=2))
        weights = jnp.exp(block - new_best[:, :, None])
        factor = jnp.exp(best - new_best)
        new_mass = mass * factor + jnp.sum(weights, axis=2)
        new_sums = sums * factor[:, :, None] + jnp.einsum("hqk,khd->hqd", weights, piece_values)
        return (new_best, new_mass, new_sums)

    node_start = my_nodes * SLOT
    touched = jnp.any((node_start + SLOT > start) & (node_start < start + count))
    top, total, accum = lax.cond(touched, absorb, lambda state: state, (top, total, accum))
    attn = (accum / total[:, :, None]).astype(jnp.bfloat16)
    partial_value = jnp.einsum(
        "hqd,hdm->qm",
        attn,
        out_weight.reshape(heads_here, HD, D),
        preferred_element_type=jnp.float32,
    )
    tp_index = lax.axis_index("tp")
    tp_count = lax.axis_size("tp")
    half = D // tp_count
    experts = w_gate.shape[0] * lax.axis_size("seq")
    cap = 5 * rows * TOPK // (4 * experts)
    dest = slot_plan(expert_ids, experts, cap)
    hidden_state = layer_input.astype(jnp.float32) + lax.psum(partial_value, "tp")
    mean_square = jnp.mean(hidden_state * hidden_state, axis=1, keepdims=True)
    normed = (hidden_state * lax.rsqrt(mean_square + 1e-06) * norm_gain).astype(jnp.bfloat16)
    spread = jnp.repeat(normed, TOPK, axis=0)
    outgoing = (
        jnp.zeros((experts * cap, D), jnp.bfloat16).at[dest].set(spread).reshape(experts, cap, D)
    )
    arrived = lax.all_to_all(outgoing, "seq", split_axis=0, concat_axis=0, tiled=True)
    sources = arrived.shape[0]
    items = arrived.shape[1]
    flat = arrived.reshape(sources * items, D)
    gate_part = jnp.dot(flat, w_gate[0], preferred_element_type=jnp.float32)
    up_part = jnp.dot(flat, w_up[0], preferred_element_type=jnp.float32)
    act = (jax.nn.silu(gate_part) * up_part).astype(jnp.bfloat16)
    terms = jnp.dot(act, w_down[0], preferred_element_type=jnp.float32).reshape(sources, items, D)
    summed = lax.psum_scatter(terms, "tp", scatter_dimension=2, tiled=True).astype(jnp.bfloat16)
    back = lax.all_to_all(summed, "seq", split_axis=0, concat_axis=0, tiled=True)
    residual = lax.dynamic_slice_in_dim(hidden_state, tp_index * half, half, 1)
    results = back.reshape(experts * cap, half)[dest].reshape(rows, TOPK, half).astype(jnp.float32)
    mixture = jnp.sum(gates[:, :, None] * results, axis=1)
    return (residual + mixture).astype(jnp.bfloat16)


def solution(mesh):
    in_specs = (
        P("seq", None),
        P("seq", "tp"),
        P(None, "seq", "tp"),
        P(None, "seq", "tp"),
        P(),
        P("seq", None),
        P("tp", None),
        P(),
        P("seq", None),
        P("seq", None),
        P("seq", None, "tp"),
        P("seq", None, "tp"),
        P("seq", "tp", None),
    )
    out_specs = P("seq", "tp")
    return jax.shard_map(local, mesh=mesh, in_specs=in_specs, out_specs=out_specs, check_vma=False)
```

profile of v0, /device:TPU:32, one launch (start us, length us, event | category | flops | bytes accessed | tf_op | source)
XLA Modules:
  0.0 488.0 jit_solution(6804841801555121420)
XLA Ops:
  6.5 1.9 copy.61
  8.5 2.1 fusion.37
  10.5 1.1 copy.78
  11.6 1.2 copy.54
  12.8 1.2 copy.79
  14.1 0.6 and_reduce_fusion
  15.4 1.5 multiply_reduce_fusion.1
  16.9 0.4 fusion.28
  17.3 1.6 fusion.27
  18.9 71.8 %all-gather.2.cloned.1.call-done = bf16[2,2048,1024]{2,0,1:T(2,128)(2,1)} async-done(((bf16[2,32,1024]{2,0,1:T(2,128)(2,1)}), bf16[2,2048,1024]{2,0,1:T(2,128)(2,1)}) %all-gather.2.cloned.1.call-update) | async-done | bytes 8388624 | tf_op jit(solution)/shard_map/all_gather | solution.py:51
  90.7 39.8 %conditional.1 = ((f32[8,256]{1,0:T(8,128)S(1)}, f32[8,256,128]{2,1,0:T(8,128)})) conditional(s32[]{:T(128)} %convert_element_type.35, (f32[8,256]{1,0:T(8,128)S(1)}, f32[8,256,128]{2,1,0:T(8,128)}) %tuple.12, (s32[64]{0:T(128)S(1)}, s32[64]{0:T(128)S(1)}, s32[1,3]{1,0:T(1,128)S(1)}, bf16[2,2048,1024]{2,0,1:T(2,128)(2,1)}, ...), branch_computations={%region_3.0_spmd, %region_4.9_spmd} | conditional | flops 2190389248 | bytes 95064616 | solution.py:79
  90.7 0.1 select_reduce_fusion
  90.9 0.1 compare_reduce_fusion
  91.0 21.2 %copy.62 = bf16[2,2048,1024]{1,2,0:T(8,128)(2,1)} copy(bf16[2,2048,1024]{2,0,1:T(2,128)(2,1)} %get-tuple-element.58) | data formatting | bytes 16777216 | tf_op jit(solution)/shard_map
  112.2 5.2 %fusion.36 = (bf16[1,2048,1024]{1,2,0:T(8,128)(2,1)}, bf16[1,2048,1024]{1,2,0:T(8,128)(2,1)S(1)}) fusion(bf16[2,2048,1024]{1,2,0:T(8,128)(2,1)} %copy.62), kind=kLoop, calls=%fused_computation.69 | loop fusion | bytes 16777216 | tf_op jit(solution)/shard_map/cond/branch_1_fun/slice | solution.py:64
  117.4 2.7 fusion
  120.1 3.8 fusion.2
  123.9 6.7 %fusion.7 = f32[8,256,128]{2,1,0:T(8,128)} fusion(bf16[2048,8,128]{0,2,1:T(8,128)(2,1)} %bitcast.63, f32[8,256,2048]{2,1,0:T(8,128)S(1)} %get-tuple-element.70, f32[8,256]{1,0:T(8,128)S(1)} %max.2, pred[2048]{0:T(1024)(128)(4,1)S(1)} %fusion.14, f32[8,256,128]{2,1,0:T(8,128)} %get-tuple-element.32, f32[8,256]{1,0:T(8,128)S(1)} %get-tuple-element.64), kind=kOutput, calls=%fused_computation.11 | convolution fusion | flops 1086849024 | bytes 23087104 | tf_op jit(solution)/shard_map/cond/branch_1_fun/hqk,khd->hqd/dot_general | solution.py:74
  130.6 5.2 %convolution_bitcast_fusion = f32[256,2048]{1,0:T(8,128)} fusion(bf16[8,128,2048]{2,1,0:T(8,128)(2,1)} %bitcast.73, f32[8,256,128]{2,1,0:T(8,128)} %get-tuple-element.35, f32[8,256]{1,0:T(8,128)S(1)} %get-tuple-element.36), kind=kOutput, calls=%fused_computation.37 | convolution fusion | flops 1074266112 | bytes 7348224 | tf_op jit(solution)/shard_map/hqd,hdm->qm/dot_general | solution.py:81
  135.8 0.5 reduce-scatter.2.cloned.1.call-start
  136.3 0.1 copy.66
  136.4 0.1 eq.59
  136.5 0.1 eq.55
  136.7 18.1 %reduce-window.6 = s32[64,16,128]{2,1,0:T(8,128)S(1)} reduce-window(s32[64,16,128]{2,1,0:T(8,128)S(1)} %fusion.34, s32[]{:T(128)} %constant.69.clone.1), window={size=1x1x128 pad=0_0x0_0x127_0}, to_apply=%region_10.11 | reduce-window | flops 16646144 | bytes 1048580 | tf_op jit(solution)/shard_map/reduce-window
  154.8 0.2 slice.26
  155.0 0.4 copy.77
  155.5 0.2 reduce-window.9
  155.7 0.1 copy.65
  155.8 0.1 mul.87
  155.9 0.2 broadcast_add_fusion
  156.1 0.2 fusion.32
  156.4 6.3 %all-reduce.2.cloned.1.call-done = f32[256,2048]{1,0:T(8,128)} async-done(((f32[256,2048]{1,0:T(8,128)}), f32[256,2048]{1,0:T(8,128)}) %all-reduce.2.cloned.1.call-update) | async-done | bytes 2097168 | tf_op jit(solution)/shard_map/psum | solution.py:93
  162.7 2.2 multiply_reduce_fusion
  164.9 1.3 copy-done.1
  166.3 0.2 multiply_convert_fusion.1
  166.5 18.1 %scatter_custom_fusion = bf16[2560,2048]{1,0:T(8,128)(2,1)} fusion(s32[2048]{0:T(1024)S(1)} %bitcast.69, bf16[]{:T(256)} %constant.77.clone.1, bf16[256,2048]{1,0:T(8,128)(2,1)S(1)} %multiply_convert_fusion.1), kind=kCustom, calls=%fused_computation.32 | custom fusion | bytes 11534338 | tf_op jit(solution)/shard_map/scatter | solution.py:98
  184.6 128.9 %all_to_all.10 = bf16[64,40,2048]{2,1,0:T(8,128)(2,1)S(1)} all-to-all(bf16[64,40,2048]{2,1,0:T(8,128)(2,1)} %bitcast.57), channel_id=1, replica_groups=mesh['seq'=64,'tp'=2] {'seq'}, dimensions={0} | all-to-all | bytes 20971520 | tf_op jit(solution)/shard_map/all_to_all | solution.py:100
  313.4 5.7 %fusion.25 = f32[2560,512]{1,0:T(8,128)S(1)} fusion(bf16[2560,2048]{1,0:T(8,128)(2,1)S(1)} %bitcast.59, bf16[1,2048,512]{2,1,0:T(8,128)(2,1)S(1)} %copy-done.8), kind=kOutput, calls=%fused_computation.41 | convolution fusion | flops 5368709120 | bytes 17825792 | tf_op jit(solution)/shard_map/dot_general | solution.py:104
  319.1 6.7 %multiply_convert_fusion = bf16[2560,512]{1,0:T(8,128)(2,1)S(1)} fusion(f32[2560,512]{1,0:T(8,128)S(1)} %fusion.25, bf16[2560,2048]{1,0:T(8,128)(2,1)S(1)} %bitcast.60, bf16[1,2048,512]{2,1,0:T(8,128)(2,1)S(1)} %copy-done.9), kind=kOutput, calls=%fused_computation.34 | convolution fusion | flops 5376573440 | bytes 20447232 | tf_op jit(solution)/shard_map/dot_general | solution.py:105
  325.8 9.9 %fusion.22 = f32[64,40,2048]{2,1,0:T(8,128)} fusion(bf16[64,40,512]{2,1,0:T(8,128)(2,1)S(1)} %bitcast.74, bf16[1,512,2048]{2,1,0:T(8,128)(2,1)S(1)} %copy-done), kind=kOutput, calls=%fused_computation.38 | convolution fusion | flops 5368709120 | bytes 25690112 | tf_op jit(solution)/shard_map/dot_general | solution.py:107
  335.7 37.4 %reduce-scatter.2.cloned.1.call-done = f32[64,40,1024]{2,1,0:T(8,128)} async-done(((f32[64,40,2048]{2,1,0:T(8,128)}), f32[64,40,1024]{2,1,0:T(8,128)}) %reduce-scatter.2.cloned.1.call-update) | async-done | bytes 10485776 | tf_op jit(solution)/shard_map/reduce_scatter | solution.py:108
  373.1 7.2 %convert_element_type.40 = bf16[64,40,1024]{2,1,0:T(8,128)(2,1)} convert(f32[64,40,1024]{2,1,0:T(8,128)} %reduce-scatter.2.cloned.1.call-done) | non-fusion elementwise | flops 2621440 | bytes 15728640 | tf_op jit(solution)/shard_map/convert_element_type | solution.py:108
  380.2 11.0 %all-to-all-start.1 = ((bf16[64,40,1024]{2,1,0:T(8,128)(2,1)}), bf16[64,40,1024]{2,1,0:T(8,128)(2,1)}, u32[]{:S(2)}, u32[]{:S(2)}) async-start(bf16[64,40,1024]{2,1,0:T(8,128)(2,1)} %convert_element_type.40), calls=%async_computation.2 | async-start | bytes 10485760 | tf_op jit(solution)/shard_map/all_to_all | solution.py:109
  391.3 0.1 copy.64
  391.4 69.8 %all-to-all-done.1 = bf16[64,40,1024]{2,1,0:T(8,128)(2,1)} async-done(((bf16[64,40,1024]{2,1,0:T(8,128)(2,1)}), bf16[64,40,1024]{2,1,0:T(8,128)(2,1)}, u32[]{:S(2)}, u32[]{:S(2)}) %all-to-all-start.1) | async-done | bytes 5242912 | tf_op jit(solution)/shard_map/all_to_all | solution.py:109
  461.2 14.2 %gather_fusion = bf16[2048,1024]{1,0:T(8,128)(2,1)} fusion(bf16[2560,1024]{1,0:T(8,128)(2,1)} %bitcast.21, s32[2048]{0:T(1024)S(1)} %broadcast_clamp_fusion), kind=kCustom, calls=%fused_computation | custom fusion | bytes 8396800 | tf_op jit(solution)/shard_map/gather | solution.py:111
  475.4 4.9 %fusion.17 = f32[256,1024]{1,0:T(8,128)S(1)} fusion(bf16[2048,1024]{1,0:T(8,128)(2,1)} %gather_fusion, f32[256,8]{1,0:T(8,128)S(1)} %copy.64), kind=kLoop, calls=%fused_computation.31 | loop fusion | flops 6029312 | bytes 5251072 | tf_op jit(solution)/shard_map/reduce_sum | solution.py:112
  480.3 0.9 add_convert_fusion
  (35 shorter events, 0.2 us)
Async XLA Ops:
  6.5 319.2 %copy-start = (bf16[1,512,2048]{2,1,0:T(8,128)(2,1)S(1)}, bf16[1,512,2048]{2,1,0:T(8,128)(2,1)}, u32[]{:S(2)}) copy-start(bf16[1,512,2048]{2,1,0:T(8,128)(2,1)} %param.27) | copy-start | bytes 6291460
  6.5 7.5 %copy-start.7 = (s32[1,3]{1,0:T(1,128)S(1)}, s32[1,3]{1,0:T(1,128)}, u32[]{:S(2)}) copy-start(s32[1,3]{1,0:T(1,128)} %param.20) | copy-start | bytes 40
  6.5 84.2 %all-gather.2.cloned.1.call-start = ((), (), s32[]{:S(2)}) async-start(), calls=%async_computation.3 | async-start | bytes 8519680 | tf_op jit(solution)/shard_map/all_gather | solution.py:51
  8.4 154.3 %all-reduce.2.cloned.1.call-start = ((), (), s32[]{:S(2)}) async-start(), calls=%async_computation.4 | async-start | bytes 4194304 | tf_op jit(solution)/shard_map/psum | solution.py:93
  15.4 75.4 %copy-start.6 = (s32[64]{0:T(128)S(1)}, s32[64]{0:T(128)}, u32[]{:S(2)}) copy-start(s32[64]{0:T(128)} %param.19) | copy-start | bytes 772
  130.6 5.7 %copy-start.3 = (s32[256,8]{0,1:T(8,128)S(1)}, s32[256,8]{0,1:T(8,128)}, u32[]{:S(2)}) copy-start(s32[256,8]{0,1:T(8,128)} %param.23) | copy-start | bytes 24580
  135.8 237.3 %reduce-scatter.2.cloned.1.call-start = ((), (), s32[]{:S(2)}) async-start(), calls=%async_computation.5 | async-start | bytes 31457280 | tf_op jit(solution)/shard_map/reduce_scatter | solution.py:108
  154.8 11.4 %copy-start.4 = (f32[2048]{0:T(1024)S(1)}, f32[2048]{0:T(1024)}, u32[]{:S(2)}) copy-start(f32[2048]{0:T(1024)} %param.22) | copy-start | bytes 24580
  164.9 1.3 copy-start.1
  184.6 128.9 %copy-start.8 = (bf16[1,2048,512]{2,1,0:T(8,128)(2,1)S(1)}, bf16[1,2048,512]{2,1,0:T(8,128)(2,1)}, u32[]{:S(2)}) copy-start(bf16[1,2048,512]{2,1,0:T(8,128)(2,1)} %param.25) | copy-start | bytes 6291460
  313.4 5.7 %copy-start.9 = (bf16[1,2048,512]{2,1,0:T(8,128)(2,1)S(1)}, bf16[1,2048,512]{2,1,0:T(8,128)(2,1)}, u32[]{:S(2)}) copy-start(bf16[1,2048,512]{2,1,0:T(8,128)(2,1)} %param.26) | copy-start | bytes 6291460
  380.2 11.0 %copy-start.5 = (f32[256,8]{0,1:T(8,128)S(1)}, f32[256,8]{0,1:T(8,128)}, u32[]{:S(2)}) copy-start(f32[256,8]{0,1:T(8,128)} %param.24) | copy-start | bytes 24580
  380.2 81.0 %all-to-all-start.1 = ((bf16[64,40,1024]{2,1,0:T(8,128)(2,1)}), bf16[64,40,1024]{2,1,0:T(8,128)(2,1)}, u32[]{:S(2)}, u32[]{:S(2)}) async-start(bf16[64,40,1024]{2,1,0:T(8,128)(2,1)} %convert_element_type.40), calls=%async_computation.2 | async-start | bytes 10485760 | tf_op jit(solution)/shard_map/all_to_all | solution.py:109
  475.4 4.9 %copy-start.2 = (f32[256,2048]{1,0:T(8,128)S(1)}, f32[256,2048]{1,0:T(8,128)}, u32[]{:S(2)}) copy-start(f32[256,2048]{1,0:T(8,128)} %copy-done.1) | copy-start | bytes 6291460
Sparse Core Ops, SparseCore 0:
  10.2 80.4 all-gather.1
  135.9 26.7 all-reduce.1
  335.8 37.2 reduce-scatter.1
where the time goes:
time: 496 us; the launch traced here: 488 us
  waiting for transfers between devices  185 us (37%)
  blocking collectives  129 us (26%)
  local copies, waits for them, and re-layouts  68.8 us (14%)
  matrix products  39.9 us (8%)
  other arithmetic  39.3 us (8%)
  between operations  14.2 us (3%)
  starting transfers between devices  11.6 us (2%)
    all_to_all x1, blocking collectives, local(): lax.all_to_all(outgoing, 'seq', split_axis=0, concat_axis=0, tiled=True)  129 us
    all_gather x1, waiting for transfers between devices, local(): piece = lax.all_gather(prefix_kv, 'seq', axis=1, tiled=True)  71.8 us
    all_to_all x1, waiting for transfers between devices, local(): lax.all_to_all(summed, 'seq', split_axis=0, concat_axis=0, tiled=True)  69.8 us
    reduce_scatter x1, waiting for transfers between devices, local(): lax.psum_scatter(terms, 'tp', scatter_dimension=2, tiled=True)  37.4 us
    another operation x2, local copies, waits for them, and re-layouts  21.7 us
    another operation x3, other arithmetic  18.5 us
    scatter x1, local copies, waits for them, and re-layouts, local(): jnp.zeros((experts * cap, D), jnp.bfloat16).at[dest].set(spread)  18.1 us
    gather x1, local copies, waits for them, and re-layouts, local(): back.reshape(experts * cap, half)[dest].reshape(rows, TOPK, half)  14.2 us
  transfers between devices with their start and end apart: 4, of which 4 were waited for; matrix products, arithmetic and copies ran while one was open for 6% of the time, Pallas kernels for 0%

commit v1 on v0

v1 whole, which is shorter than its diff:
```python
import math

import jax
import jax.numpy as jnp
from jax import lax
from jax.sharding import PartitionSpec as P

D = 2048
HD = 128
TOPK = 8


def local(
    layer_input,
    query,
    suffix_kv,
    prefix_kv,
    node_len,
    path,
    out_weight,
    norm_gain,
    expert_ids,
    gates,
    w_gate,
    w_up,
    w_down,
):
    rows = query.shape[0]
    width = query.shape[1]
    heads_here = width // HD
    scale = 1.0 / math.sqrt(HD)
    seq_count = lax.axis_size("seq")
    tp_index = lax.axis_index("tp")
    tp_count = lax.axis_size("tp")
    depth = path.shape[1]
    slot = prefix_kv.shape[1]

    gate_full = lax.all_gather(w_gate[0], "tp", axis=1, tiled=True)
    up_full = lax.all_gather(w_up[0], "tp", axis=1, tiled=True)
    down_full = lax.all_gather(w_down[0], "tp", axis=0, tiled=True)

    pieces = prefix_kv.reshape(seq_count, -1)
    piece = pieces.shape[1]
    spread = lax.all_to_all(pieces, "seq", 0, 0, tiled=True)
    paths = lax.all_to_all(
        jnp.broadcast_to(path, (seq_count, depth)), "seq", 0, 0, tiled=True
    )
    node_ids = jnp.arange(spread.shape[0], dtype=jnp.int32)
    pick = (paths.reshape(-1)[:, None] == node_ids[None, :]).astype(spread.dtype)
    picked = jnp.dot(pick, spread, preferred_element_type=jnp.float32).astype(spread.dtype)
    got = lax.all_to_all(picked.reshape(seq_count, depth * piece), "seq", 0, 0, tiled=True)
    nodes_kv = got.reshape(seq_count, depth, piece).transpose(1, 0, 2).reshape(depth, 2, slot, width)
    prefix_keys = nodes_kv[:, 0].reshape(depth * slot, heads_here, HD)
    prefix_values = nodes_kv[:, 1].reshape(depth * slot, heads_here, HD)

    my_nodes = path[0]
    lengths = jnp.sum(
        jnp.where(my_nodes[:, None] == node_ids[None, :], node_len[None, :], 0), axis=1
    )
    live = (jnp.arange(slot, dtype=jnp.int32)[None, :] < lengths[:, None]).reshape(-1)
    live_all = jnp.concatenate([jnp.ones((rows,), dtype=bool), live])

    queries = query.reshape(rows, heads_here, HD)
    keys = jnp.concatenate([suffix_kv[0].reshape(rows, heads_here, HD), prefix_keys], 0)
    values = jnp.concatenate(
        [suffix_kv[1].reshape(rows, heads_here, HD), prefix_values], 0
    ).astype(jnp.float32)
    scores = (
        jnp.einsum("qhd,khd->hqk", queries, keys, preferred_element_type=jnp.float32) * scale
    )
    scores = jnp.where(live_all[None, None, :], scores, -jnp.inf)
    top = jnp.max(scores, axis=2)
    probs = jnp.exp(scores - top[:, :, None])
    total = jnp.sum(probs, axis=2)
    accum = jnp.einsum("hqk,khd->hqd", probs, values)
    attn = (accum / total[:, :, None]).astype(jnp.bfloat16)
    partial_value = jnp.einsum(
        "hqd,hdm->qm",
        attn,
        out_weight.reshape(heads_here, HD, D),
        preferred_element_type=jnp.float32,
    )
    hidden_state = layer_input.astype(jnp.float32) + lax.psum(partial_value, "tp")
    mean_square = jnp.mean(hidden_state * hidden_state, axis=1, keepdims=True)
    normed = (hidden_state * lax.rsqrt(mean_square + 1e-06) * norm_gain).astype(jnp.bfloat16)

    experts = w_gate.shape[0] * seq_count
    cap = 5 * rows * TOPK // (4 * experts)
    share = cap // tp_count
    hit = expert_ids[:, :, None] == jnp.arange(experts, dtype=jnp.int32)[None, None, :]
    chosen = jnp.any(hit, axis=1)
    weight_of = jnp.sum(jnp.where(hit, gates[:, :, None], 0.0), axis=1)
    token = jnp.arange(rows, dtype=jnp.int32)
    earlier = (token[None, :] < token[:, None]).astype(jnp.bfloat16)
    ranks = jnp.dot(
        earlier, chosen.astype(jnp.bfloat16), preferred_element_type=jnp.float32
    ).astype(jnp.int32)
    target = tp_index * share + jnp.arange(share, dtype=jnp.int32)
    sel = chosen[:, :, None] & (ranks[:, :, None] == target[None, None, :])
    sel = sel.reshape(rows, experts * share)
    outgoing = jnp.einsum(
        "ts,td->sd", sel.astype(jnp.bfloat16), normed, preferred_element_type=jnp.float32
    ).astype(jnp.bfloat16)
    arrived = lax.all_to_all(
        outgoing.reshape(experts, share, D), "seq", 0, 0, tiled=True
    ).reshape(experts * share, D)
    gate_part = jnp.dot(arrived, gate_full, preferred_element_type=jnp.float32)
    up_part = jnp.dot(arrived, up_full, preferred_element_type=jnp.float32)
    act = (jax.nn.silu(gate_part) * up_part).astype(jnp.bfloat16)
    result = jnp.dot(act, down_full, preferred_element_type=jnp.float32).astype(jnp.bfloat16)
    back = lax.all_to_all(result.reshape(experts, share, D), "seq", 0, 0, tiled=True)
    back = back.reshape(experts * share, D)

    combine = jnp.where(sel, jnp.repeat(weight_of, share, axis=1), 0.0)
    combine_hi = combine.astype(jnp.bfloat16)
    combine_lo = (combine - combine_hi.astype(jnp.float32)).astype(jnp.bfloat16)
    mixture = jnp.dot(combine_hi, back, preferred_element_type=jnp.float32) + jnp.dot(
        combine_lo, back, preferred_element_type=jnp.float32
    )
    mixture = lax.psum_scatter(mixture, "tp", scatter_dimension=1, tiled=True)
    half = D // tp_count
    residual = lax.dynamic_slice_in_dim(hidden_state, tp_index * half, half, 1)
    return (residual + mixture).astype(jnp.bfloat16)


def solution(mesh):
    in_specs = (
        P("seq", None),
        P("seq", "tp"),
        P(None, "seq", "tp"),
        P(None, "seq", "tp"),
        P(),
        P("seq", None),
        P("tp", None),
        P(),
        P("seq", None),
        P("seq", None),
        P("seq", None, "tp"),
        P("seq", None, "tp"),
        P("seq", "tp", None),
    )
    out_specs = P("seq", "tp")
    return jax.shard_map(local, mesh=mesh, in_specs=in_specs, out_specs=out_specs, check_vma=False)
```

time: 496 us -> 401 us (0.81)
  the two profiles are of different devices: /device:TPU:32 before, /device:TPU:1 now
where the time goes in v1:
time: 401 us; the launch traced here: 395 us
  waiting for transfers between devices  226 us (56%)
  matrix products  60.8 us (15%)
  starting transfers between devices  42.1 us (10%)
  local copies, waits for them, and re-layouts  38.6 us (10%)
  between operations  13.9 us (3%)
  other arithmetic  13.5 us (3%)
    all_to_all x1, waiting for transfers between devices, local(): lax.all_to_all(outgoing.reshape(experts, share, D), 'seq', 0, 0, tiled=True)  85.9 us
    all_to_all x1, waiting for transfers between devices, local(): lax.all_to_all(result.reshape(experts, share, D), 'seq', 0, 0, tiled=True)  78.1 us
    psum x1, waiting for transfers between devices, local(): lax.psum(partial_value, 'tp')  23.6 us
    dot_general x1, matrix products, local(): jnp.dot(act, down_full, preferred_element_type=jnp.float32)  17.9 us
    reduce_scatter x1, waiting for transfers between devices, local(): mixture = lax.psum_scatter(mixture, 'tp', scatter_dimension=1, tiled=True)  17.4 us
    all_to_all x1, starting transfers between devices, local(): lax.all_to_all(jnp.broadcast_to(path, (seq_count, depth)), 'seq', 0, 0, t...  12 us
    dot_general x1, matrix products, local(): jnp.dot(combine_lo, back, preferred_element_type=jnp.float32)  10.5 us
    all_to_all x1, starting transfers between devices, local(): lax.all_to_all(outgoing.reshape(experts, share, D), 'seq', 0, 0, tiled=True)  10.3 us
  transfers between devices with their start and end apart: 10, of which 7 were waited for; matrix products, arithmetic and copies ran while one was open for 12% of the time, Pallas kernels for 0%

profile of v1, /device:TPU:1, one launch (start us, length us, event | category | flops | bytes accessed | tf_op | source)
XLA Modules:
  0.0 395.0 jit_solution(537597201021214596)
XLA Ops:
  6.5 1.3 broadcast_in_dim.46
  7.9 12.0 %all-to-all-start = ((s32[64,1,3]{2,1,0:T(1,128)}), s32[64,1,3]{2,1,0:T(1,128)S(1)}, u32[]{:S(2)}, u32[]{:S(2)}) async-start(s32[64,1,3]{2,1,0:T(1,128)} %broadcast_in_dim.46), calls=%async_computation | async-start | bytes 65536 | tf_op jit(solution)/shard_map/all_to_all | solution.py:45
  19.9 0.6 broadcast.59
  20.4 1.6 reduce.5
  22.0 0.7 reshape.106
  22.7 5.5 %all-to-all-done = s32[64,1,3]{2,1,0:T(1,128)S(1)} async-done(((s32[64,1,3]{2,1,0:T(1,128)}), s32[64,1,3]{2,1,0:T(1,128)S(1)}, u32[]{:S(2)}, u32[]{:S(2)}) %all-to-all-start) | async-done | bytes 800 | tf_op jit(solution)/shard_map/all_to_all | solution.py:45
  28.2 4.7 %all-to-all-start.1 = ((bf16[64,2,512]{2,1,0:T(2,128)(2,1)}), bf16[64,2,512]{2,1,0:T(2,128)(2,1)S(1)}, u32[]{:S(2)}, u32[]{:S(2)}) async-start(bf16[64,2,512]{2,1,0:T(2,128)(2,1)} %reshape.106), calls=%async_computation.1 | async-start | bytes 262144 | tf_op jit(solution)/shard_map/all_to_all | solution.py:44
  32.9 0.9 select_reduce_fusion.1
  33.8 0.5 broadcast.58
  34.3 0.6 reduce.4
  35.1 6.6 %all-to-all-done.1 = bf16[64,2,512]{2,1,0:T(2,128)(2,1)S(1)} async-done(((bf16[64,2,512]{2,1,0:T(2,128)(2,1)}), bf16[64,2,512]{2,1,0:T(2,128)(2,1)S(1)}, u32[]{:S(2)}, u32[]{:S(2)}) %all-to-all-start.1) | async-done | bytes 131104 | tf_op jit(solution)/shard_map/all_to_all | solution.py:44
  41.8 0.3 convolution_convert_fusion.2
  42.1 0.3 all_to_all.32
  42.5 3.0 reduce.6
  45.4 1.0 reshape.108
  46.5 5.0 %all-to-all-start.2 = ((bf16[64,2,1536]{2,1,0:T(2,128)(2,1)}), bf16[64,2,1536]{2,1,0:T(2,128)(2,1)S(1)}, u32[]{:S(2)}, u32[]{:S(2)}) async-start(bf16[64,2,1536]{2,1,0:T(2,128)(2,1)} %reshape.108), calls=%async_computation.2 | async-start | bytes 786432 | tf_op jit(solution)/shard_map/all_to_all | solution.py:51
  52.1 1.0 copy.107
  53.3 1.0 copy.112
  54.3 7.3 %all-to-all-done.2 = bf16[64,2,1536]{2,1,0:T(2,128)(2,1)S(1)} async-done(((bf16[64,2,1536]{2,1,0:T(2,128)(2,1)}), bf16[64,2,1536]{2,1,0:T(2,128)(2,1)S(1)}, u32[]{:S(2)}, u32[]{:S(2)}) %all-to-all-start.2) | async-done | bytes 393248 | tf_op jit(solution)/shard_map/all_to_all | solution.py:51
  61.6 0.3 reshape.109
  61.9 2.3 reduce.1
  64.2 0.6 reshape.83
  65.3 0.7 copy.113
  66.0 1.6 bitcast_reduce_fusion
  67.6 0.6 fusion.18
  68.3 0.4 copy-done.3
  68.7 5.7 %convolution_bitcast_fusion = f32[256,2048]{1,0:T(8,128)} fusion(bf16[8,128,2048]{2,1,0:T(8,128)(2,1)} %bitcast.81, f32[8,352,256]{2,1,0:T(8,128)S(1)} %get-tuple-element.12, f32[8,256]{1,0:T(8,128)S(1)} %get-tuple-element.11, pred[352]{0:T(512)(128)(4,1)S(1)} %concatenate.9, bf16[96,8,128]{2,0,1:T(8,128)(2,1)} %copy.113, ...), kind=kOutput, calls=%fused_computation.17 | convolution fusion | flops 1262419968 | bytes 9912672 | tf_op jit(solution)/shard_map/hqd,hdm->qm/dot_general | solution.py:77
  74.5 0.7 all-gather.7.cloned.1.call-update
  75.2 0.7 all-gather.11.cloned.1.call-update
  76.3 1.2 eq.83
  78.0 23.6 %all-reduce.3.cloned.1.call-done = f32[256,2048]{1,0:T(8,128)} async-done(((f32[256,2048]{1,0:T(8,128)}), f32[256,2048]{1,0:T(8,128)}) %all-reduce.3.cloned.1.call-update) | async-done | bytes 2097168 | tf_op jit(solution)/shard_map/psum | solution.py:83
  101.5 2.2 multiply_reduce_fusion
  103.8 5.3 %convolution_convert_fusion.1 = bf16[1280,2048]{1,0:T(8,128)(2,1)} fusion(pred[256,1280]{0,1:T(32,128)(4,1)S(1)} %and.18, s32[256,1280]{0,1:T(8,128)} %eq.83, f32[256,2048]{1,0:T(8,128)S(1)} %get-tuple-element.6, f32[2048]{0:T(1024)S(1)} %copy-done.5, f32[256]{0:T(256)S(1)} %add_rsqrt_fusion, s32[1280]{0:T(1024)S(1)} %eq.85), kind=kOutput, calls=%fused_computation.1 | convolution fusion | flops 1347026944 | bytes 8992768 | tf_op jit(solution)/shard_map/ts,td->sd/dot_general | solution.py:101
  109.0 9.2 %reshape.87 = bf16[64,20,2048]{2,1,0:T(8,128)(2,1)} reshape(bf16[1280,2048]{1,0:T(8,128)(2,1)} %convolution_convert_fusion.1) | data formatting | bytes 10485760 | tf_op jit(solution)/shard_map/reshape | solution.py:105
  118.2 10.3 %all-to-all-start.3 = ((bf16[64,20,2048]{2,1,0:T(8,128)(2,1)}), bf16[64,20,2048]{2,1,0:T(8,128)(2,1)}, u32[]{:S(2)}, u32[]{:S(2)}) async-start(bf16[64,20,2048]{2,1,0:T(8,128)(2,1)} %reshape.87), calls=%async_computation.3 | async-start | bytes 12582912 | tf_op jit(solution)/shard_map/all_to_all | solution.py:104
  128.8 0.3 all-gather.9.cloned.1.call-update
  129.1 85.9 %all-to-all-done.3 = bf16[64,20,2048]{2,1,0:T(8,128)(2,1)} async-done(((bf16[64,20,2048]{2,1,0:T(8,128)(2,1)}), bf16[64,20,2048]{2,1,0:T(8,128)(2,1)}, u32[]{:S(2)}, u32[]{:S(2)}) %all-to-all-start.3) | async-done | bytes 5242912 | tf_op jit(solution)/shard_map/all_to_all | solution.py:104
  215.0 9.0 %reshape.88 = bf16[1280,2048]{1,0:T(8,128)(2,1)} reshape(bf16[64,20,2048]{2,1,0:T(8,128)(2,1)} %all-to-all-done.3) | data formatting | bytes 10485760 | tf_op jit(solution)/shard_map/reshape | solution.py:106
  224.0 10.3 %fusion.2 = f32[1280,1024]{1,0:T(8,128)} fusion(bf16[1280,2048]{1,0:T(8,128)(2,1)} %reshape.88, bf16[1,2048,1024]{2,1,0:T(8,128)(2,1)} %all-gather.7.cloned.1.call-done), kind=kOutput, calls=%fused_computation.5 | convolution fusion | flops 5368709120 | bytes 14680064 | tf_op jit(solution)/shard_map/dot_general | solution.py:107
  234.2 17.9 %convolution_convert_fusion = bf16[1280,2048]{1,0:T(8,128)(2,1)} fusion(bf16[1,1024,2048]{2,1,0:T(8,128)(2,1)} %all-gather.11.cloned.1.call-done, f32[1280,1024]{1,0:T(8,128)} %fusion.2, bf16[1280,2048]{1,0:T(8,128)(2,1)} %reshape.88, bf16[1,2048,1024]{2,1,0:T(8,128)(2,1)} %all-gather.9.cloned.1.call-done), kind=kOutput, calls=%fused_computation | convolution fusion | flops 10747904000 | bytes 24117248 | tf_op jit(solution)/shard_map/dot_general | solution.py:110
  252.1 8.9 %reshape.89 = bf16[64,20,2048]{2,1,0:T(8,128)(2,1)} reshape(bf16[1280,2048]{1,0:T(8,128)(2,1)} %convolution_convert_fusion) | data formatting | bytes 10485760 | tf_op jit(solution)/shard_map/reshape | solution.py:111
  261.0 9.4 %all-to-all-start.4 = ((bf16[64,20,2048]{2,1,0:T(8,128)(2,1)}), bf16[64,20,2048]{2,1,0:T(8,128)(2,1)}, u32[]{:S(2)}, u32[]{:S(2)}) async-start(bf16[64,20,2048]{2,1,0:T(8,128)(2,1)} %reshape.89), calls=%async_computation.4 | async-start | bytes 12582912 | tf_op jit(solution)/shard_map/all_to_all | solution.py:111
  270.4 0.3 reduce-scatter.2.cloned.1.call-start
  270.8 78.1 %all-to-all-done.4 = bf16[64,20,2048]{2,1,0:T(8,128)(2,1)} async-done(((bf16[64,20,2048]{2,1,0:T(8,128)(2,1)}), bf16[64,20,2048]{2,1,0:T(8,128)(2,1)}, u32[]{:S(2)}, u32[]{:S(2)}) %all-to-all-start.4) | async-done | bytes 5242912 | tf_op jit(solution)/shard_map/all_to_all | solution.py:111
  348.8 9.1 %fusion.9 = f32[256,2048]{1,0:T(8,128)S(1)} fusion(bf16[64,20,2048]{2,1,0:T(8,128)(2,1)} %all-to-all-done.4, f32[256,64]{0,1:T(8,128)S(1)} %select_reduce_fusion, s32[256,64]{0,1:T(8,128)S(1)} %convolution_convert_fusion.3, s32[20]{0:T(128)S(1)} %iota_add_fusion, pred[256,64]{0,1:T(8,128)(4,1)S(1)} %fusion.64), kind=kOutput, calls=%fused_computation.15 | convolution fusion | flops 1343160320 | bytes 7487568 | tf_op jit(solution)/shard_map/dot_general | solution.py:117
  357.9 10.5 %fusion.15 = f32[256,2048]{1,0:T(8,128)} fusion(f32[256,2048]{1,0:T(8,128)S(1)} %fusion.9, bf16[64,20,2048]{2,1,0:T(8,128)(2,1)} %all-to-all-done.4, f32[256,64]{0,1:T(8,128)S(1)} %select_reduce_fusion, s32[256,64]{0,1:T(8,128)S(1)} %convolution_convert_fusion.3, s32[20]{0:T(128)S(1)} %iota_add_fusion, pred[256,64]{0,1:T(8,128)(4,1)S(1)} %fusion.64), kind=kOutput, calls=%fused_computation.18 | convolution fusion | flops 1344995328 | bytes 9584720 | tf_op jit(solution)/shard_map/dot_general | solution.py:117
  368.5 17.4 %reduce-scatter.2.cloned.1.call-done = f32[256,1024]{1,0:T(8,128)} async-done(((f32[256,2048]{1,0:T(8,128)}), f32[256,1024]{1,0:T(8,128)}) %reduce-scatter.2.cloned.1.call-update) | async-done | bytes 1048592 | tf_op jit(solution)/shard_map/reduce_scatter | solution.py:120
  385.9 2.1 add_convert_fusion
  (46 shorter events, 2.7 us)
Async XLA Ops:
  6.5 59.5 %copy-start = (bf16[256,1024]{1,0:T(8,128)(2,1)S(1)}, bf16[256,1024]{1,0:T(8,128)(2,1)}, u32[]{:S(2)}) copy-start(bf16[256,1024]{1,0:T(8,128)(2,1)} %param.14) | copy-start | bytes 1572868
  7.9 20.3 %all-to-all-start = ((s32[64,1,3]{2,1,0:T(1,128)}), s32[64,1,3]{2,1,0:T(1,128)S(1)}, u32[]{:S(2)}, u32[]{:S(2)}) async-start(s32[64,1,3]{2,1,0:T(1,128)} %broadcast_in_dim.46), calls=%async_computation | async-start | bytes 65536 | tf_op jit(solution)/shard_map/all_to_all | solution.py:45
  19.9 32.0 %copy-start.2 = (bf16[2,256,1024]{2,1,0:T(8,128)(2,1)S(1)}, bf16[2,256,1024]{2,1,0:T(8,128)(2,1)}, u32[]{:S(2)}) copy-start(bf16[2,256,1024]{2,1,0:T(8,128)(2,1)} %param.15) | copy-start | bytes 3145732
  28.2 13.5 %all-to-all-start.1 = ((bf16[64,2,512]{2,1,0:T(2,128)(2,1)}), bf16[64,2,512]{2,1,0:T(2,128)(2,1)S(1)}, u32[]{:S(2)}, u32[]{:S(2)}) async-start(bf16[64,2,512]{2,1,0:T(2,128)(2,1)} %reshape.106), calls=%async_computation.1 | async-start | bytes 262144 | tf_op jit(solution)/shard_map/all_to_all | solution.py:44
  46.5 15.1 %all-to-all-start.2 = ((bf16[64,2,1536]{2,1,0:T(2,128)(2,1)}), bf16[64,2,1536]{2,1,0:T(2,128)(2,1)S(1)}, u32[]{:S(2)}, u32[]{:S(2)}) async-start(bf16[64,2,1536]{2,1,0:T(2,128)(2,1)} %reshape.108), calls=%async_computation.2 | async-start | bytes 786432 | tf_op jit(solution)/shard_map/all_to_all | solution.py:51
  51.4 50.1 %all-reduce.3.cloned.1.call-start = ((), (), s32[]{:S(2)}) async-start(), calls=%async_computation.6 | async-start | bytes 4194304 | tf_op jit(solution)/shard_map/psum | solution.py:83
  67.6 1.0 copy-start.3
  74.4 1.5 copy-start.4
  74.4 149.6 %all-gather.7.cloned.1.call-start = ((), (), s32[]{:S(2)}) async-start(), calls=%async_computation.8 | async-start | bytes 6291456 | tf_op jit(solution)/shard_map/all_gather | solution.py:38
  75.2 159.1 %all-gather.11.cloned.1.call-start = ((), (), s32[]{:S(2)}) async-start(), calls=%async_computation.10 | async-start | bytes 6291456 | tf_op jit(solution)/shard_map/all_gather | solution.py:40
  77.7 26.1 %copy-start.5 = (f32[2048]{0:T(1024)S(1)}, f32[2048]{0:T(1024)}, u32[]{:S(2)}) copy-start(f32[2048]{0:T(1024)} %param.20) | copy-start | bytes 24580
  118.2 96.8 %all-to-all-start.3 = ((bf16[64,20,2048]{2,1,0:T(8,128)(2,1)}), bf16[64,20,2048]{2,1,0:T(8,128)(2,1)}, u32[]{:S(2)}, u32[]{:S(2)}) async-start(bf16[64,20,2048]{2,1,0:T(8,128)(2,1)} %reshape.87), calls=%async_computation.3 | async-start | bytes 12582912 | tf_op jit(solution)/shard_map/all_to_all | solution.py:104
  128.5 105.7 %all-gather.9.cloned.1.call-start = ((), (), s32[]{:S(2)}) async-start(), calls=%async_computation.9 | async-start | bytes 6291456 | tf_op jit(solution)/shard_map/all_gather | solution.py:39
  261.0 9.7 %copy-start.6 = (f32[256,8]{0,1:T(8,128)S(1)}, f32[256,8]{0,1:T(8,128)}, u32[]{:S(2)}) copy-start(f32[256,8]{0,1:T(8,128)} %param.22) | copy-start | bytes 24580
  261.0 87.8 %all-to-all-start.4 = ((bf16[64,20,2048]{2,1,0:T(8,128)(2,1)}), bf16[64,20,2048]{2,1,0:T(8,128)(2,1)}, u32[]{:S(2)}, u32[]{:S(2)}) async-start(bf16[64,20,2048]{2,1,0:T(8,128)(2,1)} %reshape.89), calls=%async_computation.4 | async-start | bytes 12582912 | tf_op jit(solution)/shard_map/all_to_all | solution.py:111
  270.4 115.5 %reduce-scatter.2.cloned.1.call-start = ((), (), s32[]{:S(2)}) async-start(), calls=%async_computation.7 | async-start | bytes 3145728 | tf_op jit(solution)/shard_map/reduce_scatter | solution.py:120
  357.9 30.1 %copy-start.1 = (bf16[256,1024]{1,0:T(8,128)(2,1)S(1)}, bf16[256,1024]{1,0:T(8,128)(2,1)}, u32[]{:S(2)}) copy-start(bf16[256,1024]{1,0:T(8,128)(2,1)} %param.14) | copy-start | bytes 1572868
Sparse Core Ops, SparseCore 0:
  74.5 26.9 all-reduce.2
  103.3 17.7 all-gather.6
  122.8 17.6 all-gather.10
  142.1 17.6 all-gather.8
  368.6 17.2 reduce-scatter.1

commit v2 on v1

--- a/solution.py
+++ b/solution.py
@@ -41,10 +41,12 @@
 
     pieces = prefix_kv.reshape(seq_count, -1)
     piece = pieces.shape[1]
-    spread = lax.all_to_all(pieces, "seq", 0, 0, tiled=True)
-    paths = lax.all_to_all(
-        jnp.broadcast_to(path, (seq_count, depth)), "seq", 0, 0, tiled=True
+    tag = jnp.zeros((seq_count, 128), pieces.dtype).at[:, :depth].set(
+        jnp.broadcast_to(path.astype(pieces.dtype), (seq_count, depth))
     )
+    spread = lax.all_to_all(jnp.concatenate([pieces, tag], 1), "seq", 0, 0, tiled=True)
+    paths = spread[:, piece : piece + depth].astype(jnp.int32)
+    spread = spread[:, :piece]
     node_ids = jnp.arange(spread.shape[0], dtype=jnp.int32)
     pick = (paths.reshape(-1)[:, None] == node_ids[None, :]).astype(spread.dtype)
     picked = jnp.dot(pick, spread, preferred_element_type=jnp.float32).astype(spread.dtype)
@@ -86,7 +88,7 @@
 
     experts = w_gate.shape[0] * seq_count
     cap = 5 * rows * TOPK // (4 * experts)
-    share = cap // tp_count
+    share = -(-(-(-cap // tp_count)) // 8) * 8
     hit = expert_ids[:, :, None] == jnp.arange(experts, dtype=jnp.int32)[None, None, :]
     chosen = jnp.any(hit, axis=1)
     weight_of = jnp.sum(jnp.where(hit, gates[:, :, None], 0.0), axis=1)
@@ -95,11 +97,11 @@
     ranks = jnp.dot(
         earlier, chosen.astype(jnp.bfloat16), preferred_element_type=jnp.float32
     ).astype(jnp.int32)
-    target = tp_index * share + jnp.arange(share, dtype=jnp.int32)
+    target = tp_count * jnp.arange(share, dtype=jnp.int32) + tp_index
     sel = chosen[:, :, None] & (ranks[:, :, None] == target[None, None, :])
-    sel = sel.reshape(rows, experts * share)
+    sel = sel.reshape(rows, experts * share).astype(jnp.bfloat16)
     outgoing = jnp.einsum(
-        "ts,td->sd", sel.astype(jnp.bfloat16), normed, preferred_element_type=jnp.float32
+        "ts,td->sd", sel, normed, preferred_element_type=jnp.float32
     ).astype(jnp.bfloat16)
     arrived = lax.all_to_all(
         outgoing.reshape(experts, share, D), "seq", 0, 0, tiled=True
@@ -107,18 +109,34 @@
     gate_part = jnp.dot(arrived, gate_full, preferred_element_type=jnp.float32)
     up_part = jnp.dot(arrived, up_full, preferred_element_type=jnp.float32)
     act = (jax.nn.silu(gate_part) * up_part).astype(jnp.bfloat16)
-    result = jnp.dot(act, down_full, preferred_element_type=jnp.float32).astype(jnp.bfloat16)
-    back = lax.all_to_all(result.reshape(experts, share, D), "seq", 0, 0, tiled=True)
-    back = back.reshape(experts * share, D)
+    half = D // tp_count
+    result = jnp.einsum(
+        "sf,fuc->usc",
+        act,
+        down_full.reshape(down_full.shape[0], tp_count, half),
+        preferred_element_type=jnp.float32,
+    ).astype(jnp.bfloat16)
+    back = lax.all_to_all(
+        result.reshape(tp_count * experts, share, half), ("tp", "seq"), 0, 0, tiled=True
+    )
+    back = back.reshape(tp_count * experts * share, half)
 
-    combine = jnp.where(sel, jnp.repeat(weight_of, share, axis=1), 0.0)
+    spot = (
+        tp_count * jnp.arange(share, dtype=jnp.int32)[None, None, :]
+        + jnp.arange(tp_count, dtype=jnp.int32)[:, None, None]
+    )
+    combine = jnp.where(
+        chosen.T[None, :, :, None] & (ranks.T[None, :, :, None] == spot[:, None, :, :]),
+        weight_of.T[None, :, :, None],
+        0.0,
+    )
+    combine = jnp.moveaxis(combine, 2, 0).reshape(rows, -1)
     combine_hi = combine.astype(jnp.bfloat16)
     combine_lo = (combine - combine_hi.astype(jnp.float32)).astype(jnp.bfloat16)
+    combine_hi, combine_lo = lax.optimization_barrier((combine_hi, combine_lo))
     mixture = jnp.dot(combine_hi, back, preferred_element_type=jnp.float32) + jnp.dot(
         combine_lo, back, preferred_element_type=jnp.float32
     )
-    mixture = lax.psum_scatter(mixture, "tp", scatter_dimension=1, tiled=True)
-    half = D // tp_count
     residual = lax.dynamic_slice_in_dim(hidden_state, tp_index * half, half, 1)
     return (residual + mixture).astype(jnp.bfloat16)
 

time: 401 us -> 336 us (0.84); the launches traced: 395 us -> 335 us
  local copies, waits for them, and re-layouts: 38.6 us -> 12.3 us
  waiting for transfers between devices: 226 us -> 200 us
  matrix products: 60.8 us -> 55.5 us
  starting transfers between devices: 42.1 us -> 37.3 us
    reshape x3 -> x0, local copies, waits for them, and re-layouts: 27.1 us -> none  [the longest x1 9.15 us: local(): outgoing.reshape(experts, share, D)]
    reduce_scatter x1 -> x0, waiting for transfers between devices: 17.4 us -> none  [local(): mixture = lax.psum_scatter(mixture, 'tp', scatter_dimension=1, tiled=True)]
    dot_general x1, matrix products: 10.5 us -> 5.51 us  [local(): jnp.dot(combine_lo, back, preferred_element_type=jnp.float32)]
    all_to_all x3 -> x2, waiting for transfers between devices: 90.1 us -> 85.4 us  [the longest x1 77.3 us: local(): lax.all_to_all(result.reshape(tp_count * experts, share, half), ('tp', 's...]
    all_to_all x3 -> x2, starting transfers between devices: 26 us -> 21.4 us  [the longest x1 12.1 us: local(): lax.all_to_all(jnp.concatenate([pieces, tag], 1), 'seq', 0, 0, tiled=True)]
    unnamed x24 -> x28, local copies, waits for them, and re-layouts: 3.22 us -> 7.45 us
  transfers between devices with their start and end apart: 10 -> 8, of which waited for: 7 -> 5; matrix products, arithmetic and copies ran while one was open for 12% -> 9% of each run, Pallas kernels for 0% -> 0%
where the time goes in v2:
time: 336 us; the launch traced here: 335 us
  waiting for transfers between devices  200 us (60%)
  matrix products  55.5 us (17%)
  starting transfers between devices  37.3 us (11%)
  other arithmetic  17 us (5%)
  between operations  13.5 us (4%)
  local copies, waits for them, and re-layouts  12.3 us (4%)
    all_to_all x1, waiting for transfers between devices, local(): lax.all_to_all(outgoing.reshape(experts, share, D), 'seq', 0, 0, tiled=True)  82.1 us
    all_to_all x1, waiting for transfers between devices, local(): lax.all_to_all(result.reshape(tp_count * experts, share, half), ('tp', 's...  77.3 us
    psum x1, waiting for transfers between devices, local(): lax.psum(partial_value, 'tp')  24.1 us
    dot_general x1, matrix products, local(): jnp.einsum('sf,fuc->usc', act, down_full.reshape(down_full.shape[0], tp_c...  20.6 us
    all_to_all x1, starting transfers between devices, local(): lax.all_to_all(jnp.concatenate([pieces, tag], 1), 'seq', 0, 0, tiled=True)  12.1 us
    dot_general x1, matrix products, local(): gate_part = jnp.dot(arrived, gate_full, preferred_element_type=jnp.float32)  11.7 us
    all_to_all x1, starting transfers between devices, local(): lax.all_to_all(outgoing.reshape(experts, share, D), 'seq', 0, 0, tiled=True)  10.4 us
    all_to_all x1, starting transfers between devices, local(): lax.all_to_all(result.reshape(tp_count * experts, share, half), ('tp', 's...  9.3 us
  transfers between devices with their start and end apart: 8, of which 5 were waited for; matrix products, arithmetic and copies ran while one was open for 9% of the time, Pallas kernels for 0%

profile of v2, /device:TPU:1, one launch (start us, length us, event | category | flops | bytes accessed | tf_op | source)
XLA Modules:
  0.0 335.5 jit_solution(14727653574408771465)
XLA Ops:
  6.5 0.6 compare_reduce_fusion
  7.2 1.3 fusion.50
  8.5 0.9 maximum_bitcast_fusion
  9.4 0.6 broadcast.135
  10.0 0.7 reduce.9
  10.8 0.9 reshape.148
  11.6 12.1 %all-to-all-start = ((bf16[64,2,576]{2,1,0:T(2,128)(2,1)}), bf16[64,2,576]{2,1,0:T(2,128)(2,1)S(1)}, u32[]{:S(2)}, u32[]{:S(2)}) async-start(bf16[64,2,576]{2,1,0:T(2,128)(2,1)} %reshape.148), calls=%async_computation | async-start | bytes 327680 | tf_op jit(solution)/shard_map/all_to_all | solution.py:47
  23.7 0.9 select_reduce_fusion.1
  24.6 8.1 %all-to-all-done = bf16[64,2,576]{2,1,0:T(2,128)(2,1)S(1)} async-done(((bf16[64,2,576]{2,1,0:T(2,128)(2,1)}), bf16[64,2,576]{2,1,0:T(2,128)(2,1)S(1)}, u32[]{:S(2)}, u32[]{:S(2)}) %all-to-all-start) | async-done | bytes 147488 | tf_op jit(solution)/shard_map/all_to_all | solution.py:47
  32.6 0.2 reshape.149
  33.1 0.3 convolution_convert_fusion.2
  33.4 0.3 all_to_all.27
  33.7 3.0 reduce.10
  36.7 1.0 reshape.150
  37.8 5.0 %all-to-all-start.1 = ((bf16[64,2,1536]{2,1,0:T(2,128)(2,1)}), bf16[64,2,1536]{2,1,0:T(2,128)(2,1)S(1)}, u32[]{:S(2)}, u32[]{:S(2)}) async-start(bf16[64,2,1536]{2,1,0:T(2,128)(2,1)} %reshape.150), calls=%async_computation.1 | async-start | bytes 786432 | tf_op jit(solution)/shard_map/all_to_all | solution.py:53
  42.7 0.2 all-reduce.4.cloned.1.call-start
  43.2 0.2 copy.97
  43.4 1.0 copy.86
  44.4 0.2 copy.99
  44.6 1.0 copy.91
  45.6 7.3 %all-to-all-done.1 = bf16[64,2,1536]{2,1,0:T(2,128)(2,1)S(1)} async-done(((bf16[64,2,1536]{2,1,0:T(2,128)(2,1)}), bf16[64,2,1536]{2,1,0:T(2,128)(2,1)S(1)}, u32[]{:S(2)}, u32[]{:S(2)}) %all-to-all-start.1) | async-done | bytes 393248 | tf_op jit(solution)/shard_map/all_to_all | solution.py:53
  52.9 0.3 reshape.151
  53.3 2.3 reduce.7
  55.6 0.6 reshape.130
  56.6 0.7 copy.92
  57.3 1.6 bitcast_reduce_fusion
  59.0 0.6 fusion.13
  59.6 0.4 copy-done.4
  60.0 5.7 %convolution_bitcast_fusion = f32[256,2048]{1,0:T(8,128)} fusion(bf16[8,128,2048]{2,1,0:T(8,128)(2,1)} %bitcast.127, f32[8,352,256]{2,1,0:T(8,128)S(1)} %get-tuple-element.28, f32[8,256]{1,0:T(8,128)S(1)} %get-tuple-element.27, pred[352]{0:T(512)(128)(4,1)S(1)} %concatenate.14, bf16[96,8,128]{2,0,1:T(8,128)(2,1)} %copy.92, ...), kind=kOutput, calls=%fused_computation.17 | convolution fusion | flops 1262419968 | bytes 9912672 | tf_op jit(solution)/shard_map/hqd,hdm->qm/dot_general | solution.py:79
  65.8 0.7 all-gather.7.cloned.1.call-update
  66.7 0.2 convolution_convert_fusion.3
  66.9 0.3 fusion.16
  67.2 24.1 %all-reduce.4.cloned.1.call-done = f32[256,2048]{1,0:T(8,128)} async-done(((f32[256,2048]{1,0:T(8,128)}), f32[256,2048]{1,0:T(8,128)}) %all-reduce.4.cloned.1.call-update) | async-done | bytes 2097168 | tf_op jit(solution)/shard_map/psum | solution.py:85
  91.4 2.2 multiply_reduce_fusion
  93.6 4.6 %convolution_convert_fusion = bf16[1536,2048]{1,0:T(8,128)(2,1)} fusion(pred[256,1536]{0,1:T(32,128)(4,1)S(1)} %fusion.16, f32[256,2048]{1,0:T(8,128)S(1)} %get-tuple-element.22, f32[2048]{0:T(1024)S(1)} %copy-done.7, f32[256]{0:T(256)S(1)} %add_rsqrt_fusion), kind=kOutput, calls=%fused_computation | convolution fusion | flops 1615331328 | bytes 8791040 | tf_op jit(solution)/shard_map/ts,td->sd/dot_general | solution.py:103
  98.2 10.4 %all-to-all-start.2 = ((bf16[64,24,2048]{2,1,0:T(8,128)(2,1)}), bf16[64,24,2048]{2,1,0:T(8,128)(2,1)}, u32[]{:S(2)}, u32[]{:S(2)}) async-start(bf16[64,24,2048]{2,1,0:T(8,128)(2,1)} %bitcast.115), calls=%async_computation.2 | async-start | bytes 12582912 | tf_op jit(solution)/shard_map/all_to_all | solution.py:106
  108.6 3.9 %copy.93 = bf16[1,512,2048]{1,2,0:T(8,128)(2,1)} copy(bf16[1,512,2048]{2,1,0:T(8,128)(2,1)} %param.27) | data formatting | bytes 4194304 | tf_op args[12]
  112.6 0.3 all-gather.9.cloned.1.call-start
  112.9 0.3 all-gather.9.cloned.1.call-update
  113.2 82.1 %all-to-all-done.2 = bf16[64,24,2048]{2,1,0:T(8,128)(2,1)} async-done(((bf16[64,24,2048]{2,1,0:T(8,128)(2,1)}), bf16[64,24,2048]{2,1,0:T(8,128)(2,1)}, u32[]{:S(2)}, u32[]{:S(2)}) %all-to-all-start.2) | async-done | bytes 6291488 | tf_op jit(solution)/shard_map/all_to_all | solution.py:106
  195.3 11.7 %fusion.1 = f32[1536,1024]{1,0:T(8,128)} fusion(bf16[1536,2048]{1,0:T(8,128)(2,1)} %bitcast.18, bf16[1,2048,1024]{2,1,0:T(8,128)(2,1)} %all-gather.7.cloned.1.call-done), kind=kOutput, calls=%fused_computation.4 | convolution fusion | flops 6442450944 | bytes 16777216 | tf_op jit(solution)/shard_map/dot_general | solution.py:109
  207.0 20.6 %convolution_convert_fusion.1 = bf16[1536,2,1024]{2,0,1:T(8,128)(2,1)} fusion(bf16[1024,2,1024]{0,2,1:T(8,128)(2,1)} %bitcast.128, bf16[1536,2048]{1,0:T(8,128)(2,1)} %bitcast.18, bf16[1,2048,1024]{2,1,0:T(8,128)(2,1)} %all-gather.9.cloned.1.call-done, f32[1536,1024]{1,0:T(8,128)} %fusion.1), kind=kOutput, calls=%fused_computation.2 | convolution fusion | flops 12897484800 | bytes 27262976 | tf_op jit(solution)/shard_map/sf,fuc->usc/dot_general | solution.py:113
  227.6 9.3 %all-to-all-start.3 = ((bf16[128,24,1024]{2,1,0:T(8,128)(2,1)}), bf16[128,24,1024]{2,1,0:T(8,128)(2,1)}, u32[]{:S(2)}, u32[]{:S(2)}) async-start(bf16[128,24,1024]{2,1,0:T(8,128)(2,1)} %bitcast.116), calls=%async_computation.3 | async-start | bytes 12582912 | tf_op jit(solution)/shard_map/all_to_all | solution.py:119
  237.1 1.9 fusion.8
  239.0 1.9 fusion.7
  240.9 77.3 %all-to-all-done.3 = bf16[128,24,1024]{2,1,0:T(8,128)(2,1)} async-done(((bf16[128,24,1024]{2,1,0:T(8,128)(2,1)}), bf16[128,24,1024]{2,1,0:T(8,128)(2,1)}, u32[]{:S(2)}, u32[]{:S(2)}) %all-to-all-start.3) | async-done | bytes 6291488 | tf_op jit(solution)/shard_map/all_to_all | solution.py:119
  318.2 5.2 %fusion.61 = f32[256,1024]{1,0:T(8,128)S(1)} fusion(bf16[256,3072]{0,1:T(8,128)(2,1)} %fusion.7, bf16[3072,1024]{1,0:T(8,128)(2,1)} %bitcast.25), kind=kOutput, calls=%fused_computation.77 | convolution fusion | flops 1610612736 | bytes 8912896 | tf_op jit(solution)/shard_map/dot_general | solution.py:137
  323.4 5.5 %fusion.22 = bf16[256,1024]{1,0:T(8,128)(2,1)} fusion(f32[256,1024]{1,0:T(8,128)S(1)} %fusion.61, bf16[256,3072]{0,1:T(8,128)(2,1)S(1)} %copy-done.2, bf16[3072,1024]{1,0:T(8,128)(2,1)} %bitcast.25, f32[256,2048]{1,0:T(8,128)S(1)} %get-tuple-element.22, s32[]{:T(128)S(6)} %select_n.27), kind=kOutput, calls=%fused_computation.31 | convolution fusion | flops 1611399168 | bytes 10485764 | tf_op jit(solution)/shard_map/dot_general | solution.py:137
  (46 shorter events, 1.3 us)
Async XLA Ops:
  6.5 50.8 %copy-start = (bf16[256,1024]{1,0:T(8,128)(2,1)S(1)}, bf16[256,1024]{1,0:T(8,128)(2,1)}, u32[]{:S(2)}) copy-start(bf16[256,1024]{1,0:T(8,128)(2,1)} %param.16) | copy-start | bytes 1572868
  11.6 31.5 %copy-start.3 = (bf16[2,256,1024]{2,1,0:T(8,128)(2,1)S(1)}, bf16[2,256,1024]{2,1,0:T(8,128)(2,1)}, u32[]{:S(2)}) copy-start(bf16[2,256,1024]{2,1,0:T(8,128)(2,1)} %param.17) | copy-start | bytes 3145732
  11.6 21.0 %all-to-all-start = ((bf16[64,2,576]{2,1,0:T(2,128)(2,1)}), bf16[64,2,576]{2,1,0:T(2,128)(2,1)S(1)}, u32[]{:S(2)}, u32[]{:S(2)}) async-start(bf16[64,2,576]{2,1,0:T(2,128)(2,1)} %reshape.148), calls=%async_computation | async-start | bytes 327680 | tf_op jit(solution)/shard_map/all_to_all | solution.py:47
  37.8 15.2 %all-to-all-start.1 = ((bf16[64,2,1536]{2,1,0:T(2,128)(2,1)}), bf16[64,2,1536]{2,1,0:T(2,128)(2,1)S(1)}, u32[]{:S(2)}, u32[]{:S(2)}) async-start(bf16[64,2,1536]{2,1,0:T(2,128)(2,1)} %reshape.150), calls=%async_computation.1 | async-start | bytes 786432 | tf_op jit(solution)/shard_map/all_to_all | solution.py:53
  42.7 48.6 %all-reduce.4.cloned.1.call-start = ((), (), s32[]{:S(2)}) async-start(), calls=%async_computation.4 | async-start | bytes 4194304 | tf_op jit(solution)/shard_map/psum | solution.py:85
  58.9 1.0 copy-start.4
  65.7 0.9 copy-start.5
  65.7 47.5 %all-gather.7.cloned.1.call-start = ((), (), s32[]{:S(2)}) async-start(), calls=%async_computation.5 | async-start | bytes 6291456 | tf_op jit(solution)/shard_map/all_gather | solution.py:38
  66.9 26.7 %copy-start.7 = (f32[2048]{0:T(1024)S(1)}, f32[2048]{0:T(1024)}, u32[]{:S(2)}) copy-start(f32[2048]{0:T(1024)} %param.22) | copy-start | bytes 24580
  98.2 97.1 %all-to-all-start.2 = ((bf16[64,24,2048]{2,1,0:T(8,128)(2,1)}), bf16[64,24,2048]{2,1,0:T(8,128)(2,1)}, u32[]{:S(2)}, u32[]{:S(2)}) async-start(bf16[64,24,2048]{2,1,0:T(8,128)(2,1)} %bitcast.115), calls=%async_computation.2 | async-start | bytes 12582912 | tf_op jit(solution)/shard_map/all_to_all | solution.py:106
  108.6 98.4 %all-gather.11.cloned.1.call-start = ((), (), s32[]{:S(2)}) async-start(), calls=%async_computation.7 | async-start | bytes 6291456 | tf_op jit(solution)/shard_map/all_gather | solution.py:40
  112.6 94.4 %all-gather.9.cloned.1.call-start = ((), (), s32[]{:S(2)}) async-start(), calls=%async_computation.6 | async-start | bytes 6291456 | tf_op jit(solution)/shard_map/all_gather | solution.py:39
  227.6 9.4 %copy-start.6 = (f32[256,8]{0,1:T(8,128)S(1)}, f32[256,8]{0,1:T(8,128)}, u32[]{:S(2)}) copy-start(f32[256,8]{0,1:T(8,128)} %param.24) | copy-start | bytes 24580
  227.6 90.6 %all-to-all-start.3 = ((bf16[128,24,1024]{2,1,0:T(8,128)(2,1)}), bf16[128,24,1024]{2,1,0:T(8,128)(2,1)}, u32[]{:S(2)}, u32[]{:S(2)}) async-start(bf16[128,24,1024]{2,1,0:T(8,128)(2,1)} %bitcast.116), calls=%async_computation.3 | async-start | bytes 12582912 | tf_op jit(solution)/shard_map/all_to_all | solution.py:119
  318.2 5.2 %copy-start.2 = (bf16[256,3072]{0,1:T(8,128)(2,1)S(1)}, bf16[256,3072]{0,1:T(8,128)(2,1)}, u32[]{:S(2)}) copy-start(bf16[256,3072]{0,1:T(8,128)(2,1)} %fusion.8) | copy-start | bytes 4718596
  323.4 5.5 %copy-start.1 = (bf16[256,1024]{1,0:T(8,128)(2,1)S(1)}, bf16[256,1024]{1,0:T(8,128)(2,1)}, u32[]{:S(2)}) copy-start(bf16[256,1024]{1,0:T(8,128)(2,1)} %param.16) | copy-start | bytes 1572868
Sparse Core Ops, SparseCore 0:
  65.8 25.4 all-reduce.3
  93.1 17.7 all-gather.6
  112.7 17.8 all-gather.10
  132.2 17.6 all-gather.8

commit v3 on v2

--- a/solution.py
+++ b/solution.py
@@ -35,9 +35,10 @@
     depth = path.shape[1]
     slot = prefix_kv.shape[1]
 
-    gate_full = lax.all_gather(w_gate[0], "tp", axis=1, tiled=True)
-    up_full = lax.all_gather(w_up[0], "tp", axis=1, tiled=True)
-    down_full = lax.all_gather(w_down[0], "tp", axis=0, tiled=True)
+    swap = [(i, (i + 1) % tp_count) for i in range(tp_count)]
+    gate_full = jnp.concatenate([w_gate[0], lax.ppermute(w_gate[0], "tp", swap)], 1)
+    up_full = jnp.concatenate([w_up[0], lax.ppermute(w_up[0], "tp", swap)], 1)
+    down_full = jnp.concatenate([w_down[0], lax.ppermute(w_down[0], "tp", swap)], 0)
 
     pieces = prefix_kv.reshape(seq_count, -1)
     piece = pieces.shape[1]
@@ -82,7 +83,8 @@
         out_weight.reshape(heads_here, HD, D),
         preferred_element_type=jnp.float32,
     )
-    hidden_state = layer_input.astype(jnp.float32) + lax.psum(partial_value, "tp")
+    heads_sum = partial_value + lax.ppermute(partial_value, "tp", swap)
+    hidden_state = layer_input.astype(jnp.float32) + heads_sum
     mean_square = jnp.mean(hidden_state * hidden_state, axis=1, keepdims=True)
     normed = (hidden_state * lax.rsqrt(mean_square + 1e-06) * norm_gain).astype(jnp.bfloat16)
 
@@ -133,10 +135,9 @@
     combine = jnp.moveaxis(combine, 2, 0).reshape(rows, -1)
     combine_hi = combine.astype(jnp.bfloat16)
     combine_lo = (combine - combine_hi.astype(jnp.float32)).astype(jnp.bfloat16)
-    combine_hi, combine_lo = lax.optimization_barrier((combine_hi, combine_lo))
-    mixture = jnp.dot(combine_hi, back, preferred_element_type=jnp.float32) + jnp.dot(
-        combine_lo, back, preferred_element_type=jnp.float32
-    )
+    both = lax.optimization_barrier(jnp.concatenate([combine_hi, combine_lo], 0))
+    parts = jnp.dot(both, back, preferred_element_type=jnp.float32)
+    mixture = parts[:rows] + parts[rows:]
     residual = lax.dynamic_slice_in_dim(hidden_state, tp_index * half, half, 1)
     return (residual + mixture).astype(jnp.bfloat16)
 

time: 336 us -> 307 us (0.914)
  waiting for transfers between devices: 200 us -> 179 us
  between operations: 13.5 us -> 0.38 us
  local copies, waits for them, and re-layouts: 12.3 us -> 24.9 us
  matrix products: 55.5 us -> 47.8 us
    psum x1 -> x0, waiting for transfers between devices: 24.1 us -> none  [local(): lax.psum(partial_value, 'tp')]
    dot_general x1, matrix products: 20.6 us -> 8.77 us  [local(): jnp.einsum('sf,fuc->usc', act, down_full.reshape(down_full.shape[0], tp_c...]
    convert_element_type x0 -> x1, local copies, waits for them, and re-layouts: none -> 8.67 us  [local(): result = jnp.einsum('sf,fuc->usc', act, down_full.reshape(down_full.shape...]
    dot_general x2, matrix products: 10.7 us -> 16.5 us  [the longest x1 9.96 us: local(): up_part = jnp.dot(arrived, up_full, preferred_element_type=jnp.float32)]
    all_to_all x1, starting transfers between devices: 10.4 us -> 5.69 us  [local(): lax.all_to_all(outgoing.reshape(experts, share, D), 'seq', 0, 0, tiled=True)]
    ppermute x0 -> x4, starting transfers between devices: none -> 4.3 us  [the longest x1 3.12 us: local(): heads_sum = partial_value + lax.ppermute(partial_value, 'tp', swap)]
    ppermute x0 -> x1, local copies, waits for them, and re-layouts: none -> 3.92 us  [local(): lax.ppermute(w_down[0], 'tp', swap)]
    ppermute x0 -> x4, waiting for transfers between devices: none -> 3.39 us  [the longest x1 3.38 us: local(): heads_sum = partial_value + lax.ppermute(partial_value, 'tp', swap)]
  transfers between devices with their start and end apart: 8 -> 8, of which waited for: 5 -> 5; matrix products, arithmetic and copies ran while one was open for 9% -> 8% of each run, Pallas kernels for 0% -> 0%
where the time goes in v3:
time: 307 us; the launch traced here: 306 us
  waiting for transfers between devices  179 us (58%)
  matrix products  47.8 us (16%)
  starting transfers between devices  36.4 us (12%)
  local copies, waits for them, and re-layouts  24.9 us (8%)
  other arithmetic  18.3 us (6%)
    all_to_all x1, waiting for transfers between devices, local(): lax.all_to_all(outgoing.reshape(experts, share, D), 'seq', 0, 0, tiled=True)  82 us
    all_to_all x1, waiting for transfers between devices, local(): lax.all_to_all(result.reshape(tp_count * experts, share, half), ('tp', 's...  77.7 us
    all_to_all x1, starting transfers between devices, local(): lax.all_to_all(jnp.concatenate([pieces, tag], 1), 'seq', 0, 0, tiled=True)  12.1 us
    dot_general x1, matrix products, local(): gate_part = jnp.dot(arrived, gate_full, preferred_element_type=jnp.float32)  10.2 us
    dot_general x1, matrix products, local(): up_part = jnp.dot(arrived, up_full, preferred_element_type=jnp.float32)  9.96 us
    all_to_all x1, starting transfers between devices, local(): lax.all_to_all(result.reshape(tp_count * experts, share, half), ('tp', 's...  9.15 us
    dot_general x1, matrix products, local(): jnp.einsum('sf,fuc->usc', act, down_full.reshape(down_full.shape[0], tp_c...  8.77 us
    convert_element_type x1, local copies, waits for them, and re-layouts, local(): result = jnp.einsum('sf,fuc->usc', act, down_full.reshape(down_full.shape...  8.67 us
  transfers between devices with their start and end apart: 8, of which 5 were waited for; matrix products, arithmetic and copies ran while one was open for 8% of the time, Pallas kernels for 0%

profile of v3, /device:TPU:1, one launch (start us, length us, event | category | flops | bytes accessed | tf_op | source)
XLA Modules:
  0.0 306.4 jit_solution(7073734871915461347)
XLA Ops:
  0.0 0.6 compare_reduce_fusion
  0.6 1.3 fusion.58
  2.0 0.9 maximum_bitcast_fusion
  2.9 0.6 broadcast.135
  3.5 0.7 reduce.9
  4.2 0.9 reshape.144
  5.1 12.1 %all-to-all-start = ((bf16[64,2,576]{2,1,0:T(2,128)(2,1)}), bf16[64,2,576]{2,1,0:T(2,128)(2,1)S(1)}, u32[]{:S(2)}, u32[]{:S(2)}) async-start(bf16[64,2,576]{2,1,0:T(2,128)(2,1)} %reshape.144), calls=%async_computation | async-start | bytes 327680 | tf_op jit(solution)/shard_map/all_to_all | solution.py:48
  17.2 0.9 select_reduce_fusion.1
  18.0 8.1 %all-to-all-done = bf16[64,2,576]{2,1,0:T(2,128)(2,1)S(1)} async-done(((bf16[64,2,576]{2,1,0:T(2,128)(2,1)}), bf16[64,2,576]{2,1,0:T(2,128)(2,1)S(1)}, u32[]{:S(2)}, u32[]{:S(2)}) %all-to-all-start) | async-done | bytes 147488 | tf_op jit(solution)/shard_map/all_to_all | solution.py:48
  26.1 0.2 reshape.145
  26.5 0.3 convolution_convert_fusion.1
  26.8 0.3 all_to_all.27
  27.2 3.0 reduce.10
  30.2 1.0 reshape.146
  31.2 5.1 %all-to-all-start.1 = ((bf16[64,2,1536]{2,1,0:T(2,128)(2,1)}), bf16[64,2,1536]{2,1,0:T(2,128)(2,1)S(1)}, u32[]{:S(2)}, u32[]{:S(2)}) async-start(bf16[64,2,1536]{2,1,0:T(2,128)(2,1)} %reshape.146), calls=%async_computation.1 | async-start | bytes 786432 | tf_op jit(solution)/shard_map/all_to_all | solution.py:54
  36.8 1.0 copy.93
  38.0 1.0 copy.98
  39.0 7.4 %all-to-all-done.1 = bf16[64,2,1536]{2,1,0:T(2,128)(2,1)S(1)} async-done(((bf16[64,2,1536]{2,1,0:T(2,128)(2,1)}), bf16[64,2,1536]{2,1,0:T(2,128)(2,1)S(1)}, u32[]{:S(2)}, u32[]{:S(2)}) %all-to-all-start.1) | async-done | bytes 393248 | tf_op jit(solution)/shard_map/all_to_all | solution.py:54
  46.4 0.3 reshape.147
  46.7 2.3 reduce.7
  49.0 0.6 reshape.131
  50.1 0.7 copy.99
  50.8 1.6 bitcast_reduce_fusion
  52.4 0.7 fusion.21
  53.1 0.4 copy-done.5
  53.5 5.7 %convolution_bitcast_fusion = f32[256,2048]{1,0:T(8,128)} fusion(bf16[8,128,2048]{2,1,0:T(8,128)(2,1)} %bitcast.120, f32[8,352,256]{2,1,0:T(8,128)S(1)} %get-tuple-element.24, f32[8,256]{1,0:T(8,128)S(1)} %get-tuple-element.23, pred[352]{0:T(512)(128)(4,1)S(1)} %concatenate.31, bf16[96,8,128]{2,0,1:T(8,128)(2,1)} %copy.99, ...), kind=kOutput, calls=%fused_computation.26 | convolution fusion | flops 1262419968 | bytes 9912672 | tf_op jit(solution)/shard_map/hqd,hdm->qm/dot_general | solution.py:80
  59.2 3.1 %collective-permute-start = (f32[256,2048]{1,0:T(8,128)}, f32[256,2048]{1,0:T(8,128)}, u32[]{:S(2)}, u32[]{:S(2)}) collective-permute-start(f32[256,2048]{1,0:T(8,128)} %convolution_bitcast_fusion), channel_id=1, source_target_pairs={{0,1},{1,0},{2,3},{3,2},{4,5},{5,4},{6,7},{7,6},{8,9},{9,8},{10,11... | collective-permute-start | bytes 6291464 | tf_op jit(solution)/shard_map/ppermute | solution.py:86
  62.7 0.3 fusion.24
  63.1 3.4 %collective-permute-done = f32[256,2048]{1,0:T(8,128)} collective-permute-done((f32[256,2048]{1,0:T(8,128)}, f32[256,2048]{1,0:T(8,128)}, u32[]{:S(2)}, u32[]{:S(2)}) %collective-permute-start) | collective-permute-done | bytes 2097184 | tf_op jit(solution)/shard_map/ppermute | solution.py:86
  66.4 2.9 multiply_reduce_fusion
  69.4 4.6 %convolution_convert_fusion = bf16[1536,2048]{1,0:T(8,128)(2,1)} fusion(pred[256,1536]{0,1:T(32,128)(4,1)S(1)} %fusion.24, f32[256,2048]{1,0:T(8,128)S(1)} %get-tuple-element.18, f32[2048]{0:T(1024)S(1)} %copy-done.8, f32[256]{0:T(256)S(1)} %add_rsqrt_fusion), kind=kOutput, calls=%fused_computation | convolution fusion | flops 1615331328 | bytes 8791040 | tf_op jit(solution)/shard_map/ts,td->sd/dot_general | solution.py:105
  73.9 5.7 %all-to-all-start.2 = ((bf16[64,24,2048]{2,1,0:T(8,128)(2,1)}), bf16[64,24,2048]{2,1,0:T(8,128)(2,1)}, u32[]{:S(2)}, u32[]{:S(2)}) async-start(bf16[64,24,2048]{2,1,0:T(8,128)(2,1)} %bitcast.105), calls=%async_computation.2 | async-start | bytes 12582912 | tf_op jit(solution)/shard_map/all_to_all | solution.py:108
  79.6 0.7 collective-permute-start.1
  80.4 0.4 collective-permute-start.3
  80.8 3.9 %copy.100 = bf16[1,512,2048]{1,2,0:T(8,128)(2,1)} copy(bf16[1,512,2048]{2,1,0:T(8,128)(2,1)} %param.27) | data formatting | bytes 4194304 | tf_op args[12]
  84.8 3.9 %copy.101 = bf16[512,2048]{0,1:T(8,128)(2,1)} copy(bf16[512,2048]{1,0:T(8,128)(2,1)} %collective-permute-done.1) | data formatting | bytes 4194304 | tf_op jit(solution)/shard_map/ppermute | solution.py:41
  88.7 82.0 %all-to-all-done.2 = bf16[64,24,2048]{2,1,0:T(8,128)(2,1)} async-done(((bf16[64,24,2048]{2,1,0:T(8,128)(2,1)}), bf16[64,24,2048]{2,1,0:T(8,128)(2,1)}, u32[]{:S(2)}, u32[]{:S(2)}) %all-to-all-start.2) | async-done | bytes 6291488 | tf_op jit(solution)/shard_map/all_to_all | solution.py:108
  170.7 10.2 %fusion.3 = f32[1536,1024]{1,0:T(8,128)S(1)} fusion(bf16[1536,2048]{1,0:T(8,128)(2,1)} %bitcast.21, bf16[2048,512]{1,0:T(8,128)(2,1)} %collective-permute-done.2, bf16[2048,512]{1,0:T(8,128)(2,1)} %bitcast.122), kind=kOutput, calls=%fused_computation.6 | convolution fusion | flops 6450839552 | bytes 16777216 | tf_op jit(solution)/shard_map/dot_general | solution.py:111
  180.9 10.0 %fusion.13 = bf16[1536,1024,1]{1,0,2:T(8,128)(2,1)S(1)} fusion(bf16[1536,2048]{1,0:T(8,128)(2,1)} %bitcast.21, bf16[2048,512]{1,0:T(8,128)(2,1)} %collective-permute-done.3, bf16[2048,512]{1,0:T(8,128)(2,1)S(1)} %bitcast.124, f32[1536,1024]{1,0:T(8,128)S(1)} %fusion.3), kind=kOutput, calls=%fused_computation.14 | convolution fusion | flops 6460276736 | bytes 19922944 | tf_op jit(solution)/shard_map/dot_general | solution.py:112
  190.9 8.8 %convert_bitcast_fusion = bf16[2,1536,1024]{1,2,0:T(8,128)(2,1)} fusion(bf16[1536,1024,1]{1,0,2:T(8,128)(2,1)S(1)} %fusion.13, bf16[512,2,1024]{0,2,1:T(8,128)(2,1)S(1)} %bitcast.110, bf16[512,2,1024]{0,2,1:T(8,128)(2,1)S(1)} %bitcast.109), kind=kOutput, calls=%fused_computation.1 | convolution fusion | flops 6453985280 | bytes 13631488 | tf_op jit(solution)/shard_map/sf,fuc->usc/dot_general | solution.py:115
  199.6 8.7 %copy.102 = bf16[2,1536,1024]{2,1,0:T(8,128)(2,1)} copy(bf16[2,1536,1024]{1,2,0:T(8,128)(2,1)} %convert_bitcast_fusion) | data formatting | bytes 12582912 | tf_op jit(solution)/shard_map/convert_element_type | solution.py:120
  208.3 9.1 %all-to-all-start.3 = ((bf16[128,24,1024]{2,1,0:T(8,128)(2,1)}), bf16[128,24,1024]{2,1,0:T(8,128)(2,1)}, u32[]{:S(2)}, u32[]{:S(2)}) async-start(bf16[128,24,1024]{2,1,0:T(8,128)(2,1)} %bitcast.106), calls=%async_computation.3 | async-start | bytes 12582912 | tf_op jit(solution)/shard_map/all_to_all | solution.py:121
  217.7 0.6 fusion.17
  218.3 0.7 fusion.18
  219.1 1.9 pad_maximum_fusion
  221.0 77.7 %all-to-all-done.3 = bf16[128,24,1024]{2,1,0:T(8,128)(2,1)} async-done(((bf16[128,24,1024]{2,1,0:T(8,128)(2,1)}), bf16[128,24,1024]{2,1,0:T(8,128)(2,1)}, u32[]{:S(2)}, u32[]{:S(2)}) %all-to-all-start.3) | async-done | bytes 6291488 | tf_op jit(solution)/shard_map/all_to_all | solution.py:121
  298.7 6.6 %fusion.71 = f32[512,1024]{1,0:T(8,128)S(1)} fusion(bf16[512,3072]{0,1:T(8,128)(2,1)} %pad_maximum_fusion, bf16[3072,1024]{1,0:T(8,128)(2,1)} %bitcast.27), kind=kOutput, calls=%fused_computation.88 | convolution fusion | flops 3221225472 | bytes 11534336 | tf_op jit(solution)/shard_map/dot_general | solution.py:139
  305.3 1.1 fusion.38
  (50 shorter events, 2.0 us)
Async XLA Ops:
  0.0 50.8 %copy-start = (bf16[256,1024]{1,0:T(8,128)(2,1)S(1)}, bf16[256,1024]{1,0:T(8,128)(2,1)}, u32[]{:S(2)}) copy-start(bf16[256,1024]{1,0:T(8,128)(2,1)} %param.16) | copy-start | bytes 1572868
  5.1 31.5 %copy-start.4 = (bf16[2,256,1024]{2,1,0:T(8,128)(2,1)S(1)}, bf16[2,256,1024]{2,1,0:T(8,128)(2,1)}, u32[]{:S(2)}) copy-start(bf16[2,256,1024]{2,1,0:T(8,128)(2,1)} %param.17) | copy-start | bytes 3145732
  5.1 21.0 %all-to-all-start = ((bf16[64,2,576]{2,1,0:T(2,128)(2,1)}), bf16[64,2,576]{2,1,0:T(2,128)(2,1)S(1)}, u32[]{:S(2)}, u32[]{:S(2)}) async-start(bf16[64,2,576]{2,1,0:T(2,128)(2,1)} %reshape.144), calls=%async_computation | async-start | bytes 327680 | tf_op jit(solution)/shard_map/all_to_all | solution.py:48
  31.2 15.2 %all-to-all-start.1 = ((bf16[64,2,1536]{2,1,0:T(2,128)(2,1)}), bf16[64,2,1536]{2,1,0:T(2,128)(2,1)S(1)}, u32[]{:S(2)}, u32[]{:S(2)}) async-start(bf16[64,2,1536]{2,1,0:T(2,128)(2,1)} %reshape.146), calls=%async_computation.1 | async-start | bytes 786432 | tf_op jit(solution)/shard_map/all_to_all | solution.py:54
  52.4 1.0 copy-start.5
  53.5 9.0 %copy-start.6 = (s32[256,8]{0,1:T(8,128)S(1)}, s32[256,8]{0,1:T(8,128)}, u32[]{:S(2)}) copy-start(s32[256,8]{0,1:T(8,128)} %param.23) | copy-start | bytes 24580
  59.2 7.2 %collective-permute-start = (f32[256,2048]{1,0:T(8,128)}, f32[256,2048]{1,0:T(8,128)}, u32[]{:S(2)}, u32[]{:S(2)}) collective-permute-start(f32[256,2048]{1,0:T(8,128)} %convolution_bitcast_fusion), channel_id=1, source_target_pairs={{0,1},{1,0},{2,3},{3,2},{4,5},{5,4},{6,7},{7,6},{8,9},{9,8},{10,11... | collective-permute-start | bytes 6291464 | tf_op jit(solution)/shard_map/ppermute | solution.py:86
  63.1 6.3 %copy-start.8 = (f32[2048]{0:T(1024)S(1)}, f32[2048]{0:T(1024)}, u32[]{:S(2)}) copy-start(f32[2048]{0:T(1024)} %param.22) | copy-start | bytes 24580
  73.9 96.7 %all-to-all-start.2 = ((bf16[64,24,2048]{2,1,0:T(8,128)(2,1)}), bf16[64,24,2048]{2,1,0:T(8,128)(2,1)}, u32[]{:S(2)}, u32[]{:S(2)}) async-start(bf16[64,24,2048]{2,1,0:T(8,128)(2,1)} %bitcast.105), calls=%async_computation.2 | async-start | bytes 12582912 | tf_op jit(solution)/shard_map/all_to_all | solution.py:108
  79.6 5.1 %collective-permute-start.1 = (bf16[512,2048]{1,0:T(8,128)(2,1)}, bf16[512,2048]{1,0:T(8,128)(2,1)}, u32[]{:S(2)}, u32[]{:S(2)}) collective-permute-start(bf16[512,2048]{1,0:T(8,128)(2,1)} %bitcast.108), channel_id=1, source_target_pairs={{0,1},{1,0},{2,3},{3,2},{4,5},{5,4},{6,7},{7,6},{8,9},{9,8},{10,11... | collective-permute-start | bytes 6291464 | tf_op jit(solution)/shard_map/ppermute | solution.py:41
  80.3 8.4 %collective-permute-start.2 = (bf16[2048,512]{1,0:T(8,128)(2,1)}, bf16[2048,512]{1,0:T(8,128)(2,1)}, u32[]{:S(2)}, u32[]{:S(2)}) collective-permute-start(bf16[2048,512]{1,0:T(8,128)(2,1)} %bitcast.121), channel_id=1, source_target_pairs={{0,1},{1,0},{2,3},{3,2},{4,5},{5,4},{6,7},{7,6},{8,9},{9,8},{10,11... | collective-permute-start | bytes 6291464 | tf_op jit(solution)/shard_map/ppermute | solution.py:39
  80.4 100.4 %collective-permute-start.3 = (bf16[2048,512]{1,0:T(8,128)(2,1)}, bf16[2048,512]{1,0:T(8,128)(2,1)}, u32[]{:S(2)}, u32[]{:S(2)}) collective-permute-start(bf16[2048,512]{1,0:T(8,128)(2,1)} %bitcast.123), channel_id=1, source_target_pairs={{0,1},{1,0},{2,3},{3,2},{4,5},{5,4},{6,7},{7,6},{8,9},{9,8},{10,11... | collective-permute-start | bytes 6291464 | tf_op jit(solution)/shard_map/ppermute | solution.py:40
  170.7 10.2 %copy-start.9 = (bf16[1,2048,512]{2,1,0:T(8,128)(2,1)S(1)}, bf16[1,2048,512]{2,1,0:T(8,128)(2,1)}, u32[]{:S(2)}) copy-start(bf16[1,2048,512]{2,1,0:T(8,128)(2,1)} %param.26) | copy-start | bytes 6291460
  180.8 10.0 %copy-start.2 = (bf16[1,512,2048]{1,2,0:T(8,128)(2,1)S(1)}, bf16[1,512,2048]{1,2,0:T(8,128)(2,1)}, u32[]{:S(2)}) copy-start(bf16[1,512,2048]{1,2,0:T(8,128)(2,1)} %copy.100) | copy-start | bytes 6291460
  180.8 10.0 %copy-start.3 = (bf16[512,2048]{0,1:T(8,128)(2,1)S(1)}, bf16[512,2048]{0,1:T(8,128)(2,1)}, u32[]{:S(2)}) copy-start(bf16[512,2048]{0,1:T(8,128)(2,1)} %copy.101) | copy-start | bytes 6291460
  208.3 9.3 %copy-start.7 = (f32[256,8]{0,1:T(8,128)S(1)}, f32[256,8]{0,1:T(8,128)}, u32[]{:S(2)}) copy-start(f32[256,8]{0,1:T(8,128)} %param.24) | copy-start | bytes 24580
  208.3 90.4 %all-to-all-start.3 = ((bf16[128,24,1024]{2,1,0:T(8,128)(2,1)}), bf16[128,24,1024]{2,1,0:T(8,128)(2,1)}, u32[]{:S(2)}, u32[]{:S(2)}) async-start(bf16[128,24,1024]{2,1,0:T(8,128)(2,1)} %bitcast.106), calls=%async_computation.3 | async-start | bytes 12582912 | tf_op jit(solution)/shard_map/all_to_all | solution.py:121
  298.7 7.6 %copy-start.1 = (bf16[256,1024]{1,0:T(8,128)(2,1)S(1)}, bf16[256,1024]{1,0:T(8,128)(2,1)}, u32[]{:S(2)}) copy-start(bf16[256,1024]{1,0:T(8,128)(2,1)} %param.16) | copy-start | bytes 1572868

commit v4 on v3

--- a/solution.py
+++ b/solution.py
@@ -112,12 +112,13 @@
     up_part = jnp.dot(arrived, up_full, preferred_element_type=jnp.float32)
     act = (jax.nn.silu(gate_part) * up_part).astype(jnp.bfloat16)
     half = D // tp_count
-    result = jnp.einsum(
-        "sf,fuc->usc",
-        act,
-        down_full.reshape(down_full.shape[0], tp_count, half),
-        preferred_element_type=jnp.float32,
-    ).astype(jnp.bfloat16)
+    down_cols = down_full.reshape(down_full.shape[0], tp_count, half)
+    result = jnp.stack(
+        [
+            jnp.dot(act, down_cols[:, u], preferred_element_type=jnp.float32).astype(jnp.bfloat16)
+            for u in range(tp_count)
+        ]
+    )
     back = lax.all_to_all(
         result.reshape(tp_count * experts, share, half), ("tp", "seq"), 0, 0, tiled=True
     )

time: 307 us -> 303 us (0.987)
  local copies, waits for them, and re-layouts: 24.9 us -> 12.3 us
  other arithmetic: 18.3 us -> 21.5 us
    convert_element_type x1 -> x0, local copies, waits for them, and re-layouts: 8.67 us -> none  [local(): result = jnp.einsum('sf,fuc->usc', act, down_full.reshape(down_full.shape...]
    all_to_all x1, waiting for transfers between devices: 82 us -> 85.9 us  [local(): lax.all_to_all(outgoing.reshape(experts, share, D), 'seq', 0, 0, tiled=True)]
    ppermute x1 -> x0, local copies, waits for them, and re-layouts: 3.92 us -> none  [local(): lax.ppermute(w_down[0], 'tp', swap)]
    another operation x2 -> x3, other arithmetic: 1.94 us -> 5.14 us  [the longest x1 3.2 us: local(): jnp.stack([jnp.dot(act, down_cols[:, u], preferred_element_type=jnp.float...]
    dot_general x1 -> x2, matrix products: 8.77 us -> 9.85 us  [local(): jnp.dot(act, down_cols[:, u], preferred_element_type=jnp.float32)]
    unnamed x32 -> x30, local copies, waits for them, and re-layouts: 7.44 us -> 7.42 us
  transfers between devices with their start and end apart: 8 -> 8, of which waited for: 5 -> 5; matrix products, arithmetic and copies ran while one was open for 8% -> 10% of each run, Pallas kernels for 0% -> 0%
where the time goes in v4:
time: 303 us; the launch traced here: 302 us
  waiting for transfers between devices  182 us (60%)
  matrix products  48.9 us (16%)
  starting transfers between devices  36.4 us (12%)
  other arithmetic  21.5 us (7%)
  local copies, waits for them, and re-layouts  12.3 us (4%)
    all_to_all x1, waiting for transfers between devices, local(): lax.all_to_all(outgoing.reshape(experts, share, D), 'seq', 0, 0, tiled=True)  85.9 us
    all_to_all x1, waiting for transfers between devices, local(): lax.all_to_all(result.reshape(tp_count * experts, share, half), ('tp', 's...  77.7 us
    all_to_all x1, starting transfers between devices, local(): lax.all_to_all(jnp.concatenate([pieces, tag], 1), 'seq', 0, 0, tiled=True)  12.1 us
    dot_general x1, matrix products, local(): gate_part = jnp.dot(arrived, gate_full, preferred_element_type=jnp.float32)  10.2 us
    dot_general x1, matrix products, local(): up_part = jnp.dot(arrived, up_full, preferred_element_type=jnp.float32)  9.94 us
    dot_general x2, matrix products, local(): jnp.dot(act, down_cols[:, u], preferred_element_type=jnp.float32)  9.85 us
    all_to_all x1, starting transfers between devices, local(): lax.all_to_all(result.reshape(tp_count * experts, share, half), ('tp', 's...  9.17 us
    all_to_all x1, waiting for transfers between devices, local(): lax.all_to_all(jnp.concatenate([pieces, tag], 1), 'seq', 0, 0, tiled=True)  8.06 us
  transfers between devices with their start and end apart: 8, of which 5 were waited for; matrix products, arithmetic and copies ran while one was open for 10% of the time, Pallas kernels for 0%

profile of v4, /device:TPU:1, one launch (start us, length us, event | category | flops | bytes accessed | tf_op | source)
XLA Modules:
  0.0 302.0 jit_solution(15494989906547408530)
XLA Ops:
  0.0 0.6 compare_reduce_fusion
  0.6 1.3 fusion.60
  2.0 0.9 maximum_bitcast_fusion
  2.9 0.6 broadcast.135
  3.5 0.7 reduce.9
  4.2 0.9 reshape.143
  5.1 12.1 %all-to-all-start = ((bf16[64,2,576]{2,1,0:T(2,128)(2,1)}), bf16[64,2,576]{2,1,0:T(2,128)(2,1)S(1)}, u32[]{:S(2)}, u32[]{:S(2)}) async-start(bf16[64,2,576]{2,1,0:T(2,128)(2,1)} %reshape.143), calls=%async_computation | async-start | bytes 327680 | tf_op jit(solution)/shard_map/all_to_all | solution.py:48
  17.2 0.9 select_reduce_fusion.1
  18.0 8.1 %all-to-all-done = bf16[64,2,576]{2,1,0:T(2,128)(2,1)S(1)} async-done(((bf16[64,2,576]{2,1,0:T(2,128)(2,1)}), bf16[64,2,576]{2,1,0:T(2,128)(2,1)S(1)}, u32[]{:S(2)}, u32[]{:S(2)}) %all-to-all-start) | async-done | bytes 147488 | tf_op jit(solution)/shard_map/all_to_all | solution.py:48
  26.1 0.2 reshape.144
  26.5 0.3 convolution_convert_fusion.3
  26.8 0.3 all_to_all.27
  27.2 3.0 reduce.10
  30.2 1.0 reshape.145
  31.2 5.1 %all-to-all-start.1 = ((bf16[64,2,1536]{2,1,0:T(2,128)(2,1)}), bf16[64,2,1536]{2,1,0:T(2,128)(2,1)S(1)}, u32[]{:S(2)}, u32[]{:S(2)}) async-start(bf16[64,2,1536]{2,1,0:T(2,128)(2,1)} %reshape.145), calls=%async_computation.1 | async-start | bytes 786432 | tf_op jit(solution)/shard_map/all_to_all | solution.py:54
  36.8 1.0 copy.92
  38.0 1.0 copy.97
  39.0 7.4 %all-to-all-done.1 = bf16[64,2,1536]{2,1,0:T(2,128)(2,1)S(1)} async-done(((bf16[64,2,1536]{2,1,0:T(2,128)(2,1)}), bf16[64,2,1536]{2,1,0:T(2,128)(2,1)S(1)}, u32[]{:S(2)}, u32[]{:S(2)}) %all-to-all-start.1) | async-done | bytes 393248 | tf_op jit(solution)/shard_map/all_to_all | solution.py:54
  46.4 0.3 reshape.146
  46.7 2.3 reduce.7
  49.0 0.6 reshape.131
  50.1 0.7 copy.98
  50.8 1.6 bitcast_reduce_fusion
  52.4 0.7 fusion.17
  53.1 0.4 copy-done.4
  53.5 5.7 %convolution_bitcast_fusion = f32[256,2048]{1,0:T(8,128)} fusion(bf16[8,128,2048]{2,1,0:T(8,128)(2,1)} %bitcast.129, f32[8,352,256]{2,1,0:T(8,128)S(1)} %get-tuple-element.24, f32[8,256]{1,0:T(8,128)S(1)} %get-tuple-element.23, pred[352]{0:T(512)(128)(4,1)S(1)} %concatenate.31, bf16[96,8,128]{2,0,1:T(8,128)(2,1)} %copy.98, ...), kind=kOutput, calls=%fused_computation.28 | convolution fusion | flops 1262419968 | bytes 9912672 | tf_op jit(solution)/shard_map/hqd,hdm->qm/dot_general | solution.py:80
  59.2 3.1 %collective-permute-start = (f32[256,2048]{1,0:T(8,128)}, f32[256,2048]{1,0:T(8,128)}, u32[]{:S(2)}, u32[]{:S(2)}) collective-permute-start(f32[256,2048]{1,0:T(8,128)} %convolution_bitcast_fusion), channel_id=1, source_target_pairs={{0,1},{1,0},{2,3},{3,2},{4,5},{5,4},{6,7},{7,6},{8,9},{9,8},{10,11... | collective-permute-start | bytes 6291464 | tf_op jit(solution)/shard_map/ppermute | solution.py:86
  62.7 0.3 fusion.26
  63.1 3.4 %collective-permute-done = f32[256,2048]{1,0:T(8,128)} collective-permute-done((f32[256,2048]{1,0:T(8,128)}, f32[256,2048]{1,0:T(8,128)}, u32[]{:S(2)}, u32[]{:S(2)}) %collective-permute-start) | collective-permute-done | bytes 2097184 | tf_op jit(solution)/shard_map/ppermute | solution.py:86
  66.4 2.9 multiply_reduce_fusion
  69.4 4.6 %convolution_convert_fusion = bf16[1536,2048]{1,0:T(8,128)(2,1)} fusion(pred[256,1536]{0,1:T(32,128)(4,1)S(1)} %fusion.26, f32[256,2048]{1,0:T(8,128)S(1)} %get-tuple-element.18, f32[2048]{0:T(1024)S(1)} %copy-done.7, f32[256]{0:T(256)S(1)} %add_rsqrt_fusion), kind=kOutput, calls=%fused_computation | convolution fusion | flops 1615331328 | bytes 8791040 | tf_op jit(solution)/shard_map/ts,td->sd/dot_general | solution.py:105
  73.9 5.7 %all-to-all-start.2 = ((bf16[64,24,2048]{2,1,0:T(8,128)(2,1)}), bf16[64,24,2048]{2,1,0:T(8,128)(2,1)}, u32[]{:S(2)}, u32[]{:S(2)}) async-start(bf16[64,24,2048]{2,1,0:T(8,128)(2,1)} %bitcast.114), calls=%async_computation.2 | async-start | bytes 12582912 | tf_op jit(solution)/shard_map/all_to_all | solution.py:108
  79.6 0.7 collective-permute-start.1
  80.4 3.9 %copy.99 = bf16[1,512,2048]{1,2,0:T(8,128)(2,1)} copy(bf16[1,512,2048]{2,1,0:T(8,128)(2,1)} %param.27) | data formatting | bytes 4194304 | tf_op args[12]
  84.4 0.4 collective-permute-start.3
  84.7 85.9 %all-to-all-done.2 = bf16[64,24,2048]{2,1,0:T(8,128)(2,1)} async-done(((bf16[64,24,2048]{2,1,0:T(8,128)(2,1)}), bf16[64,24,2048]{2,1,0:T(8,128)(2,1)}, u32[]{:S(2)}, u32[]{:S(2)}) %all-to-all-start.2) | async-done | bytes 6291488 | tf_op jit(solution)/shard_map/all_to_all | solution.py:108
  170.7 10.2 %fusion = f32[1536,1024]{1,0:T(8,128)S(1)} fusion(bf16[1536,2048]{1,0:T(8,128)(2,1)} %bitcast.18, bf16[2048,512]{1,0:T(8,128)(2,1)} %collective-permute-done.1, bf16[2048,512]{1,0:T(8,128)(2,1)} %bitcast.131), kind=kOutput, calls=%fused_computation.3 | convolution fusion | flops 6450839552 | bytes 16777216 | tf_op jit(solution)/shard_map/dot_general | solution.py:111
  180.9 9.9 %multiply_convert_fusion = bf16[1536,1024]{1,0:T(8,128)(2,1)S(1)} fusion(f32[1536,1024]{1,0:T(8,128)S(1)} %fusion, bf16[1536,2048]{1,0:T(8,128)(2,1)} %bitcast.18, bf16[2048,512]{1,0:T(8,128)(2,1)} %collective-permute-done.2, bf16[2048,512]{1,0:T(8,128)(2,1)S(1)} %bitcast.133), kind=kOutput, calls=%fused_computation.2 | convolution fusion | flops 6460276736 | bytes 19922944 | tf_op jit(solution)/shard_map/dot_general | solution.py:112
  190.8 4.9 %fusion.10 = bf16[1,1536,1024]{2,1,0:T(8,128)(2,1)S(1)} fusion(bf16[1536,1024]{1,0:T(8,128)(2,1)S(1)} %multiply_convert_fusion, bf16[512,2,1024]{0,2,1:T(8,128)(2,1)S(1)} %bitcast.118, bf16[512,2,1024]{0,2,1:T(8,128)(2,1)} %bitcast.23), kind=kOutput, calls=%fused_computation.15 | convolution fusion | flops 3226992640 | bytes 10485760 | tf_op jit(solution)/shard_map/dot_general | solution.py:118
  195.8 4.9 %fusion.11 = bf16[1,1536,1024]{2,1,0:T(8,128)(2,1)S(1)} fusion(bf16[1536,1024]{1,0:T(8,128)(2,1)S(1)} %multiply_convert_fusion, bf16[512,2,1024]{0,2,1:T(8,128)(2,1)} %bitcast.23, bf16[512,2,1024]{0,2,1:T(8,128)(2,1)S(1)} %bitcast.119), kind=kOutput, calls=%fused_computation.16 | convolution fusion | flops 3226992640 | bytes 10485760 | tf_op jit(solution)/shard_map/dot_general | solution.py:118
  200.7 3.2 %pad_maximum_fusion = bf16[2,1536,1024]{2,1,0:T(8,128)(2,1)} fusion(bf16[1,1536,1024]{2,1,0:T(8,128)(2,1)S(1)} %fusion.11, bf16[1,1536,1024]{2,1,0:T(8,128)(2,1)S(1)} %fusion.10), kind=kLoop, calls=%fused_computation.1 | loop fusion | flops 3145728 | bytes 12582912 | tf_op jit(solution)/shard_map/stack | solution.py:116
  203.9 9.2 %all-to-all-start.3 = ((bf16[128,24,1024]{2,1,0:T(8,128)(2,1)}), bf16[128,24,1024]{2,1,0:T(8,128)(2,1)}, u32[]{:S(2)}, u32[]{:S(2)}) async-start(bf16[128,24,1024]{2,1,0:T(8,128)(2,1)} %bitcast.115), calls=%async_computation.3 | async-start | bytes 12582912 | tf_op jit(solution)/shard_map/all_to_all | solution.py:122
  213.3 0.6 fusion.13
  213.9 0.7 fusion.14
  214.7 1.9 pad_maximum_fusion.1
  216.6 77.7 %all-to-all-done.3 = bf16[128,24,1024]{2,1,0:T(8,128)(2,1)} async-done(((bf16[128,24,1024]{2,1,0:T(8,128)(2,1)}), bf16[128,24,1024]{2,1,0:T(8,128)(2,1)}, u32[]{:S(2)}, u32[]{:S(2)}) %all-to-all-start.3) | async-done | bytes 6291488 | tf_op jit(solution)/shard_map/all_to_all | solution.py:122
  294.4 6.6 %fusion.74 = f32[512,1024]{1,0:T(8,128)S(1)} fusion(bf16[512,3072]{0,1:T(8,128)(2,1)} %pad_maximum_fusion.1, bf16[3072,1024]{1,0:T(8,128)(2,1)} %bitcast.29), kind=kOutput, calls=%fused_computation.96 | convolution fusion | flops 3221225472 | bytes 11534336 | tf_op jit(solution)/shard_map/dot_general | solution.py:140
  300.9 1.1 fusion.40
  (48 shorter events, 2.0 us)
Async XLA Ops:
  0.0 50.8 %copy-start = (bf16[256,1024]{1,0:T(8,128)(2,1)S(1)}, bf16[256,1024]{1,0:T(8,128)(2,1)}, u32[]{:S(2)}) copy-start(bf16[256,1024]{1,0:T(8,128)(2,1)} %param.16) | copy-start | bytes 1572868
  5.1 31.5 %copy-start.3 = (bf16[2,256,1024]{2,1,0:T(8,128)(2,1)S(1)}, bf16[2,256,1024]{2,1,0:T(8,128)(2,1)}, u32[]{:S(2)}) copy-start(bf16[2,256,1024]{2,1,0:T(8,128)(2,1)} %param.17) | copy-start | bytes 3145732
  5.1 21.0 %all-to-all-start = ((bf16[64,2,576]{2,1,0:T(2,128)(2,1)}), bf16[64,2,576]{2,1,0:T(2,128)(2,1)S(1)}, u32[]{:S(2)}, u32[]{:S(2)}) async-start(bf16[64,2,576]{2,1,0:T(2,128)(2,1)} %reshape.143), calls=%async_computation | async-start | bytes 327680 | tf_op jit(solution)/shard_map/all_to_all | solution.py:48
  31.2 15.2 %all-to-all-start.1 = ((bf16[64,2,1536]{2,1,0:T(2,128)(2,1)}), bf16[64,2,1536]{2,1,0:T(2,128)(2,1)S(1)}, u32[]{:S(2)}, u32[]{:S(2)}) async-start(bf16[64,2,1536]{2,1,0:T(2,128)(2,1)} %reshape.145), calls=%async_computation.1 | async-start | bytes 786432 | tf_op jit(solution)/shard_map/all_to_all | solution.py:54
  52.4 1.0 copy-start.4
  53.5 9.0 %copy-start.5 = (s32[256,8]{0,1:T(8,128)S(1)}, s32[256,8]{0,1:T(8,128)}, u32[]{:S(2)}) copy-start(s32[256,8]{0,1:T(8,128)} %param.23) | copy-start | bytes 24580
  59.2 7.2 %collective-permute-start = (f32[256,2048]{1,0:T(8,128)}, f32[256,2048]{1,0:T(8,128)}, u32[]{:S(2)}, u32[]{:S(2)}) collective-permute-start(f32[256,2048]{1,0:T(8,128)} %convolution_bitcast_fusion), channel_id=1, source_target_pairs={{0,1},{1,0},{2,3},{3,2},{4,5},{5,4},{6,7},{7,6},{8,9},{9,8},{10,11... | collective-permute-start | bytes 6291464 | tf_op jit(solution)/shard_map/ppermute | solution.py:86
  63.1 6.3 %copy-start.7 = (f32[2048]{0:T(1024)S(1)}, f32[2048]{0:T(1024)}, u32[]{:S(2)}) copy-start(f32[2048]{0:T(1024)} %param.22) | copy-start | bytes 24580
  73.9 96.7 %all-to-all-start.2 = ((bf16[64,24,2048]{2,1,0:T(8,128)(2,1)}), bf16[64,24,2048]{2,1,0:T(8,128)(2,1)}, u32[]{:S(2)}, u32[]{:S(2)}) async-start(bf16[64,24,2048]{2,1,0:T(8,128)(2,1)} %bitcast.114), calls=%async_computation.2 | async-start | bytes 12582912 | tf_op jit(solution)/shard_map/all_to_all | solution.py:108
  79.6 5.1 %collective-permute-start.1 = (bf16[2048,512]{1,0:T(8,128)(2,1)}, bf16[2048,512]{1,0:T(8,128)(2,1)}, u32[]{:S(2)}, u32[]{:S(2)}) collective-permute-start(bf16[2048,512]{1,0:T(8,128)(2,1)} %bitcast.130), channel_id=1, source_target_pairs={{0,1},{1,0},{2,3},{3,2},{4,5},{5,4},{6,7},{7,6},{8,9},{9,8},{10,11... | collective-permute-start | bytes 6291464 | tf_op jit(solution)/shard_map/ppermute | solution.py:39
  80.3 100.5 %collective-permute-start.2 = (bf16[2048,512]{1,0:T(8,128)(2,1)}, bf16[2048,512]{1,0:T(8,128)(2,1)}, u32[]{:S(2)}, u32[]{:S(2)}) collective-permute-start(bf16[2048,512]{1,0:T(8,128)(2,1)} %bitcast.132), channel_id=1, source_target_pairs={{0,1},{1,0},{2,3},{3,2},{4,5},{5,4},{6,7},{7,6},{8,9},{9,8},{10,11... | collective-permute-start | bytes 6291464 | tf_op jit(solution)/shard_map/ppermute | solution.py:40
  84.4 106.5 %collective-permute-start.3 = (bf16[512,2048]{0,1:T(8,128)(2,1)}, bf16[512,2048]{0,1:T(8,128)(2,1)}, u32[]{:S(2)}, u32[]{:S(2)}) collective-permute-start(bf16[512,2048]{0,1:T(8,128)(2,1)} %bitcast.117), channel_id=1, source_target_pairs={{0,1},{1,0},{2,3},{3,2},{4,5},{5,4},{6,7},{7,6},{8,9},{9,8},{10,11... | collective-permute-start | bytes 6291464 | tf_op jit(solution)/shard_map/ppermute | solution.py:41
  170.7 10.2 %copy-start.8 = (bf16[1,2048,512]{2,1,0:T(8,128)(2,1)S(1)}, bf16[1,2048,512]{2,1,0:T(8,128)(2,1)}, u32[]{:S(2)}) copy-start(bf16[1,2048,512]{2,1,0:T(8,128)(2,1)} %param.26) | copy-start | bytes 6291460
  180.8 10.0 %copy-start.2 = (bf16[1,512,2048]{1,2,0:T(8,128)(2,1)S(1)}, bf16[1,512,2048]{1,2,0:T(8,128)(2,1)}, u32[]{:S(2)}) copy-start(bf16[1,512,2048]{1,2,0:T(8,128)(2,1)} %copy.99) | copy-start | bytes 6291460
  203.9 9.3 %copy-start.6 = (f32[256,8]{0,1:T(8,128)S(1)}, f32[256,8]{0,1:T(8,128)}, u32[]{:S(2)}) copy-start(f32[256,8]{0,1:T(8,128)} %param.24) | copy-start | bytes 24580
  203.9 90.5 %all-to-all-start.3 = ((bf16[128,24,1024]{2,1,0:T(8,128)(2,1)}), bf16[128,24,1024]{2,1,0:T(8,128)(2,1)}, u32[]{:S(2)}, u32[]{:S(2)}) async-start(bf16[128,24,1024]{2,1,0:T(8,128)(2,1)} %bitcast.115), calls=%async_computation.3 | async-start | bytes 12582912 | tf_op jit(solution)/shard_map/all_to_all | solution.py:122
  294.3 7.6 %copy-start.1 = (bf16[256,1024]{1,0:T(8,128)(2,1)S(1)}, bf16[256,1024]{1,0:T(8,128)(2,1)}, u32[]{:S(2)}) copy-start(bf16[256,1024]{1,0:T(8,128)(2,1)} %param.16) | copy-start | bytes 1572868

commit v5 on v4

--- a/solution.py
+++ b/solution.py
@@ -99,46 +99,53 @@
     ranks = jnp.dot(
         earlier, chosen.astype(jnp.bfloat16), preferred_element_type=jnp.float32
     ).astype(jnp.int32)
-    target = tp_count * jnp.arange(share, dtype=jnp.int32) + tp_index
-    sel = chosen[:, :, None] & (ranks[:, :, None] == target[None, None, :])
-    sel = sel.reshape(rows, experts * share).astype(jnp.bfloat16)
-    outgoing = jnp.einsum(
-        "ts,td->sd", sel, normed, preferred_element_type=jnp.float32
-    ).astype(jnp.bfloat16)
-    arrived = lax.all_to_all(
-        outgoing.reshape(experts, share, D), "seq", 0, 0, tiled=True
-    ).reshape(experts * share, D)
-    gate_part = jnp.dot(arrived, gate_full, preferred_element_type=jnp.float32)
-    up_part = jnp.dot(arrived, up_full, preferred_element_type=jnp.float32)
-    act = (jax.nn.silu(gate_part) * up_part).astype(jnp.bfloat16)
     half = D // tp_count
     down_cols = down_full.reshape(down_full.shape[0], tp_count, half)
-    result = jnp.stack(
-        [
-            jnp.dot(act, down_cols[:, u], preferred_element_type=jnp.float32).astype(jnp.bfloat16)
-            for u in range(tp_count)
-        ]
-    )
-    back = lax.all_to_all(
-        result.reshape(tp_count * experts, share, half), ("tp", "seq"), 0, 0, tiled=True
-    )
-    back = back.reshape(tp_count * experts * share, half)
+    first = max(8, share // 16 * 8)
+    mixture = None
+    for lo, hi in ((0, first), (first, share)):
+        count = hi - lo
+        target = tp_count * jnp.arange(lo, hi, dtype=jnp.int32) + tp_index
+        sel = chosen[:, :, None] & (ranks[:, :, None] == target[None, None, :])
+        sel = sel.reshape(rows, experts * count).astype(jnp.bfloat16)
+        outgoing = jnp.einsum(
+            "ts,td->sd", sel, normed, preferred_element_type=jnp.float32
+        ).astype(jnp.bfloat16)
+        arrived = lax.all_to_all(
+            outgoing.reshape(experts, count, D), "seq", 0, 0, tiled=True
+        ).reshape(experts * count, D)
+        gate_part = jnp.dot(arrived, gate_full, preferred_element_type=jnp.float32)
+        up_part = jnp.dot(arrived, up_full, preferred_element_type=jnp.float32)
+        act = (jax.nn.silu(gate_part) * up_part).astype(jnp.bfloat16)
+        result = jnp.stack(
+            [
+                jnp.dot(act, down_cols[:, u], preferred_element_type=jnp.float32).astype(
+                    jnp.bfloat16
+                )
+                for u in range(tp_count)
+            ]
+        )
+        back = lax.all_to_all(
+            result.reshape(tp_count * experts, count, half), ("tp", "seq"), 0, 0, tiled=True
+        )
+        back = back.reshape(tp_count * experts * count, half)
 
-    spot = (
-        tp_count * jnp.arange(share, dtype=jnp.int32)[None, None, :]
-        + jnp.arange(tp_count, dtype=jnp.int32)[:, None, None]
-    )
-    combine = jnp.where(
-        chosen.T[None, :, :, None] & (ranks.T[None, :, :, None] == spot[:, None, :, :]),
-        weight_of.T[None, :, :, None],
-        0.0,
-    )
-    combine = jnp.moveaxis(combine, 2, 0).reshape(rows, -1)
-    combine_hi = combine.astype(jnp.bfloat16)
-    combine_lo = (combine - combine_hi.astype(jnp.float32)).astype(jnp.bfloat16)
-    both = lax.optimization_barrier(jnp.concatenate([combine_hi, combine_lo], 0))
-    parts = jnp.dot(both, back, preferred_element_type=jnp.float32)
-    mixture = parts[:rows] + parts[rows:]
+        spot = (
+            tp_count * jnp.arange(lo, hi, dtype=jnp.int32)[None, None, :]
+            + jnp.arange(tp_count, dtype=jnp.int32)[:, None, None]
+        )
+        combine = jnp.where(
+            chosen.T[None, :, :, None] & (ranks.T[None, :, :, None] == spot[:, None, :, :]),
+            weight_of.T[None, :, :, None],
+            0.0,
+        )
+        combine = jnp.moveaxis(combine, 2, 0).reshape(rows, -1)
+        combine_hi = combine.astype(jnp.bfloat16)
+        combine_lo = (combine - combine_hi.astype(jnp.float32)).astype(jnp.bfloat16)
+        both = lax.optimization_barrier(jnp.concatenate([combine_hi, combine_lo], 0))
+        parts = jnp.dot(both, back, preferred_element_type=jnp.float32)
+        piece_sum = parts[:rows] + parts[rows:]
+        mixture = piece_sum if mixture is None else mixture + piece_sum
     residual = lax.dynamic_slice_in_dim(hidden_state, tp_index * half, half, 1)
     return (residual + mixture).astype(jnp.bfloat16)
 

time: 303 us -> 272 us (0.90); the launches traced: 302 us -> 267 us
  waiting for transfers between devices: 182 us -> 121 us
  starting transfers between devices: 36.4 us -> 52.7 us
  matrix products: 48.9 us -> 55.1 us
    all_to_all x2 -> x4, waiting for transfers between devices: 164 us -> 102 us  [the longest x2 54.1 us: local(): lax.all_to_all(outgoing.reshape(experts, count, D), 'seq', 0, 0, tiled=True)]
    all_to_all x2 -> x4, starting transfers between devices: 14.9 us -> 29.6 us  [the longest x2 17.7 us: local(): lax.all_to_all(result.reshape(tp_count * experts, count, half), ('tp', 's...]
    dot_general x1 -> x2, matrix products: 6.56 us -> 9.83 us  [local(): parts = jnp.dot(both, back, preferred_element_type=jnp.float32)]
    dot_general x1 -> x2, matrix products: 10.2 us -> 13 us  [local(): gate_part = jnp.dot(arrived, gate_full, preferred_element_type=jnp.float32)]
    dot_general x1 -> x2, matrix products: 9.94 us -> 12.7 us  [local(): up_part = jnp.dot(arrived, up_full, preferred_element_type=jnp.float32)]
    dot_general x2 -> x4, matrix products: 9.85 us -> 7.3 us  [local(): jnp.dot(act, down_cols[:, u], preferred_element_type=jnp.float32)]
    unnamed x30 -> x44, local copies, waits for them, and re-layouts: 7.42 us -> 7.48 us
  transfers between devices with their start and end apart: 8 -> 10, of which waited for: 5 -> 7; matrix products, arithmetic and copies ran while one was open for 10% -> 22% of each run, Pallas kernels for 0% -> 0%
where the time goes in v5:
time: 272 us; the launch traced here: 267 us
  waiting for transfers between devices  121 us (44%)
  matrix products  55.1 us (20%)
  starting transfers between devices  52.7 us (19%)
  other arithmetic  24.2 us (9%)
  local copies, waits for them, and re-layouts  12.5 us (5%)
    all_to_all x2, waiting for transfers between devices, local(): lax.all_to_all(outgoing.reshape(experts, count, D), 'seq', 0, 0, tiled=True)  54.1 us
    all_to_all x2, waiting for transfers between devices, local(): lax.all_to_all(result.reshape(tp_count * experts, count, half), ('tp', 's...  47.9 us
    all_to_all x2, starting transfers between devices, local(): lax.all_to_all(result.reshape(tp_count * experts, count, half), ('tp', 's...  17.7 us
    dot_general x2, matrix products, local(): gate_part = jnp.dot(arrived, gate_full, preferred_element_type=jnp.float32)  13 us
    dot_general x2, matrix products, local(): up_part = jnp.dot(arrived, up_full, preferred_element_type=jnp.float32)  12.7 us
    all_to_all x1, starting transfers between devices, local(): lax.all_to_all(jnp.concatenate([pieces, tag], 1), 'seq', 0, 0, tiled=True)  12 us
    all_to_all x2, starting transfers between devices, local(): lax.all_to_all(outgoing.reshape(experts, count, D), 'seq', 0, 0, tiled=True)  11.9 us
    dot_general x2, matrix products, local(): parts = jnp.dot(both, back, preferred_element_type=jnp.float32)  9.83 us
  transfers between devices with their start and end apart: 10, of which 7 were waited for; matrix products, arithmetic and copies ran while one was open for 22% of the time, Pallas kernels for 0%

profile of v5, /device:TPU:1, one launch (start us, length us, event | category | flops | bytes accessed | tf_op | source)
XLA Modules:
  0.0 266.7 jit_solution(12477125822765537415)
XLA Ops:
  0.6 1.3 fusion.67
  2.0 0.9 maximum_bitcast_fusion
  3.5 0.7 reduce.9
  4.2 0.9 reshape.195
  5.1 12.0 %all-to-all-start = ((bf16[64,2,576]{2,1,0:T(2,128)(2,1)}), bf16[64,2,576]{2,1,0:T(2,128)(2,1)S(1)}, u32[]{:S(2)}, u32[]{:S(2)}) async-start(bf16[64,2,576]{2,1,0:T(2,128)(2,1)} %reshape.195), calls=%async_computation | async-start | bytes 327680 | tf_op jit(solution)/shard_map/all_to_all | solution.py:48
  17.0 0.9 select_reduce_fusion.1
  17.9 8.1 %all-to-all-done = bf16[64,2,576]{2,1,0:T(2,128)(2,1)S(1)} async-done(((bf16[64,2,576]{2,1,0:T(2,128)(2,1)}), bf16[64,2,576]{2,1,0:T(2,128)(2,1)S(1)}, u32[]{:S(2)}, u32[]{:S(2)}) %all-to-all-start) | async-done | bytes 147488 | tf_op jit(solution)/shard_map/all_to_all | solution.py:48
  27.1 3.0 %reduce.10 = bf16[64,3072]{1,0:T(8,128)(2,1)S(1)} reduce(bf16[64,1,3072]{2,1,0:T(2,128)(2,1)S(1)} %all_to_all.35, bf16[]{:T(256)} %broadcast.198), dimensions={1}, to_apply=%all_to_all.35.reduce_sub_computation | reduce | bytes 786434 | tf_op jit(solution)/shard_map/all_to_all | solution.py:54
  30.1 1.0 reshape.197
  31.1 5.5 %all-to-all-start.1 = ((bf16[64,2,1536]{2,1,0:T(2,128)(2,1)}), bf16[64,2,1536]{2,1,0:T(2,128)(2,1)S(1)}, u32[]{:S(2)}, u32[]{:S(2)}) async-start(bf16[64,2,1536]{2,1,0:T(2,128)(2,1)} %reshape.197), calls=%async_computation.1 | async-start | bytes 786432 | tf_op jit(solution)/shard_map/all_to_all | solution.py:54
  37.0 1.0 copy.94
  38.3 1.0 copy.99
  39.3 7.5 %all-to-all-done.1 = bf16[64,2,1536]{2,1,0:T(2,128)(2,1)S(1)} async-done(((bf16[64,2,1536]{2,1,0:T(2,128)(2,1)}), bf16[64,2,1536]{2,1,0:T(2,128)(2,1)S(1)}, u32[]{:S(2)}, u32[]{:S(2)}) %all-to-all-start.1) | async-done | bytes 393248 | tf_op jit(solution)/shard_map/all_to_all | solution.py:54
  47.1 2.3 reduce.7
  50.5 0.7 copy.100
  52.8 5.7 %convolution_bitcast_fusion = f32[256,2048]{1,0:T(8,128)} fusion(bf16[8,128,2048]{2,1,0:T(8,128)(2,1)} %bitcast.194, f32[8,352,256]{2,1,0:T(8,128)S(1)} %get-tuple-element.24, f32[8,256]{1,0:T(8,128)S(1)} %get-tuple-element.23, pred[352]{0:T(512)(128)(4,1)S(1)} %concatenate.34, bf16[96,8,128]{2,0,1:T(8,128)(2,1)} %copy.100, ...), kind=kOutput, calls=%fused_computation.13 | convolution fusion | flops 1262419968 | bytes 9912672 | tf_op jit(solution)/shard_map/hqd,hdm->qm/dot_general | solution.py:80
  58.5 3.1 %collective-permute-start = (f32[256,2048]{1,0:T(8,128)}, f32[256,2048]{1,0:T(8,128)}, u32[]{:S(2)}, u32[]{:S(2)}) collective-permute-start(f32[256,2048]{1,0:T(8,128)} %convolution_bitcast_fusion), channel_id=1, source_target_pairs={{0,1},{1,0},{2,3},{3,2},{4,5},{5,4},{6,7},{7,6},{8,9},{9,8},{10,11... | collective-permute-start | bytes 6291464 | tf_op jit(solution)/shard_map/ppermute | solution.py:86
  62.1 3.7 %collective-permute-done = f32[256,2048]{1,0:T(8,128)} collective-permute-done((f32[256,2048]{1,0:T(8,128)}, f32[256,2048]{1,0:T(8,128)}, u32[]{:S(2)}, u32[]{:S(2)}) %collective-permute-start) | collective-permute-done | bytes 2097184 | tf_op jit(solution)/shard_map/ppermute | solution.py:86
  65.8 2.9 %multiply_reduce_fusion = (f32[256]{0:T(256)S(1)}, f32[256,2048]{1,0:T(8,128)S(1)}) fusion(f32[256,2048]{1,0:T(8,128)} %convolution_bitcast_fusion, f32[256,2048]{1,0:T(8,128)} %collective-permute-done, bf16[256,2048]{1,0:T(8,128)(2,1)} %param.15), kind=kLoop, calls=%fused_computation.39 | loop fusion | flops 2621184 | bytes 7341056 | tf_op jit(solution)/shard_map/reduce_sum | solution.py:88
  68.7 2.2 fusion.1
  70.9 5.6 %all-to-all-start.2 = ((bf16[64,8,2048]{2,1,0:T(8,128)(2,1)}), bf16[64,8,2048]{2,1,0:T(8,128)(2,1)}, u32[]{:S(2)}, u32[]{:S(2)}) async-start(bf16[64,8,2048]{2,1,0:T(8,128)(2,1)} %fusion.1), calls=%async_computation.2 | async-start | bytes 4194304 | tf_op jit(solution)/shard_map/all_to_all | solution.py:114
  77.5 3.3 %convolution_convert_fusion = bf16[1024,2048]{1,0:T(8,128)(2,1)} fusion(pred[256,1024]{0,1:T(32,128)(4,1)S(1)} %fusion.41, f32[256,2048]{1,0:T(8,128)S(1)} %get-tuple-element.18, f32[2048]{0:T(1024)S(1)} %copy-done.10, f32[256]{0:T(256)S(1)} %add_rsqrt_fusion), kind=kOutput, calls=%fused_computation.6 | convolution fusion | flops 1077411840 | bytes 6562816 | tf_op jit(solution)/shard_map/ts,td->sd/dot_general | solution.py:111
  80.8 24.3 %all-to-all-done.2 = bf16[64,8,2048]{2,1,0:T(8,128)(2,1)} async-done(((bf16[64,8,2048]{2,1,0:T(8,128)(2,1)}), bf16[64,8,2048]{2,1,0:T(8,128)(2,1)}, u32[]{:S(2)}, u32[]{:S(2)}) %all-to-all-start.2) | async-done | bytes 2097184 | tf_op jit(solution)/shard_map/all_to_all | solution.py:114
  105.1 6.4 %all-to-all-start.4 = ((bf16[64,16,2048]{2,1,0:T(8,128)(2,1)}), bf16[64,16,2048]{2,1,0:T(8,128)(2,1)}, u32[]{:S(2)}, u32[]{:S(2)}) async-start(bf16[64,16,2048]{2,1,0:T(8,128)(2,1)} %bitcast.176), calls=%async_computation.4 | async-start | bytes 8388608 | tf_op jit(solution)/shard_map/all_to_all | solution.py:114
  111.5 1.9 collective-permute-start.2
  113.4 3.9 %copy.101 = bf16[1,512,2048]{1,2,0:T(8,128)(2,1)} copy(bf16[1,512,2048]{2,1,0:T(8,128)(2,1)} %param.27) | data formatting | bytes 4194304 | tf_op args[12]
  117.3 5.3 %fusion.5 = f32[512,1024]{1,0:T(8,128)S(1)} fusion(bf16[2048,512]{1,0:T(8,128)(2,1)} %collective-permute-done.1, bf16[2048,512]{1,0:T(8,128)(2,1)} %bitcast.196, bf16[64,8,2048]{2,1,0:T(8,128)(2,1)} %all-to-all-done.2), kind=kOutput, calls=%fused_computation.17 | convolution fusion | flops 2155872256 | bytes 8388608 | tf_op jit(solution)/shard_map/dot_general | solution.py:117
  122.7 4.8 %multiply_convert_fusion.1 = bf16[512,1024]{1,0:T(8,128)(2,1)S(1)} fusion(f32[512,1024]{1,0:T(8,128)S(1)} %fusion.5, bf16[2048,512]{1,0:T(8,128)(2,1)} %collective-permute-done.2, bf16[2048,512]{1,0:T(8,128)(2,1)S(1)} %bitcast.199, bf16[64,8,2048]{2,1,0:T(8,128)(2,1)} %all-to-all-done.2), kind=kOutput, calls=%fused_computation.37 | convolution fusion | flops 2159017984 | bytes 9437184 | tf_op jit(solution)/shard_map/dot_general | solution.py:118
  127.5 1.3 fusion.25
  128.8 1.3 fusion.24
  130.1 1.5 pad_maximum_fusion.10
  131.7 29.8 %all-to-all-done.4 = bf16[64,16,2048]{2,1,0:T(8,128)(2,1)} async-done(((bf16[64,16,2048]{2,1,0:T(8,128)(2,1)}), bf16[64,16,2048]{2,1,0:T(8,128)(2,1)}, u32[]{:S(2)}, u32[]{:S(2)}) %all-to-all-start.4) | async-done | bytes 4194336 | tf_op jit(solution)/shard_map/all_to_all | solution.py:114
  161.5 10.4 %all-to-all-start.3 = ((bf16[128,8,1024]{2,1,0:T(8,128)(2,1)}), bf16[128,8,1024]{2,1,0:T(8,128)(2,1)}, u32[]{:S(2)}, u32[]{:S(2)}) async-start(bf16[128,8,1024]{2,1,0:T(8,128)(2,1)} %bitcast.178), calls=%async_computation.3 | async-start | bytes 4194304 | tf_op jit(solution)/shard_map/all_to_all | solution.py:128
  171.9 7.7 %fusion.4 = f32[1024,1024]{1,0:T(8,128)S(1)} fusion(bf16[1024,2048]{1,0:T(8,128)(2,1)} %bitcast.36, bf16[2048,512]{1,0:T(8,128)(2,1)} %collective-permute-done.1, bf16[2048,512]{1,0:T(8,128)(2,1)} %bitcast.197), kind=kOutput, calls=%fused_computation.16 | convolution fusion | flops 4303355904 | bytes 12582912 | tf_op jit(solution)/shard_map/dot_general | solution.py:117
  179.6 7.8 %multiply_convert_fusion = bf16[1024,1024]{1,0:T(8,128)(2,1)S(1)} fusion(f32[1024,1024]{1,0:T(8,128)S(1)} %fusion.4, bf16[1024,2048]{1,0:T(8,128)(2,1)} %bitcast.36, bf16[2048,512]{1,0:T(8,128)(2,1)} %collective-permute-done.2, bf16[2048,512]{1,0:T(8,128)(2,1)S(1)} %bitcast.200), kind=kOutput, calls=%fused_computation.5 | convolution fusion | flops 4309647360 | bytes 14680064 | tf_op jit(solution)/shard_map/dot_general | solution.py:118
  187.5 2.4 convert_bitcast_fusion.1
  189.9 2.4 convert_bitcast_fusion
  192.2 2.3 pad_maximum_fusion.2
  194.5 5.4 %all-to-all-done.3 = bf16[128,8,1024]{2,1,0:T(8,128)(2,1)} async-done(((bf16[128,8,1024]{2,1,0:T(8,128)(2,1)}), bf16[128,8,1024]{2,1,0:T(8,128)(2,1)}, u32[]{:S(2)}, u32[]{:S(2)}) %all-to-all-start.3) | async-done | bytes 2097184 | tf_op jit(solution)/shard_map/all_to_all | solution.py:128
  200.0 7.3 %all-to-all-start.5 = ((bf16[128,16,1024]{2,1,0:T(8,128)(2,1)}), bf16[128,16,1024]{2,1,0:T(8,128)(2,1)}, u32[]{:S(2)}, u32[]{:S(2)}) async-start(bf16[128,16,1024]{2,1,0:T(8,128)(2,1)} %bitcast.177), calls=%async_computation.5 | async-start | bytes 8388608 | tf_op jit(solution)/shard_map/all_to_all | solution.py:128
  207.8 1.1 fusion.39
  209.6 0.7 fusion.14
  210.3 1.1 pad_maximum_fusion.12
  211.4 1.5 pad_maximum_fusion.11
  212.9 4.5 %fusion.15 = f32[512,1024]{1,0:T(8,128)} fusion(bf16[512,1024]{0,1:T(8,128)(2,1)} %pad_maximum_fusion.12, bf16[128,8,1024]{2,1,0:T(8,128)(2,1)} %all-to-all-done.3), kind=kOutput, calls=%fused_computation.31 | convolution fusion | flops 1073741824 | bytes 5242880 | tf_op jit(solution)/shard_map/dot_general | solution.py:146
  217.4 42.4 %all-to-all-done.5 = bf16[128,16,1024]{2,1,0:T(8,128)(2,1)} async-done(((bf16[128,16,1024]{2,1,0:T(8,128)(2,1)}), bf16[128,16,1024]{2,1,0:T(8,128)(2,1)}, u32[]{:S(2)}, u32[]{:S(2)}) %all-to-all-start.5) | async-done | bytes 4194336 | tf_op jit(solution)/shard_map/all_to_all | solution.py:128
  259.8 5.3 %fusion.87 = f32[512,1024]{1,0:T(8,128)S(1)} fusion(bf16[512,2048]{0,1:T(8,128)(2,1)} %pad_maximum_fusion.11, bf16[2048,1024]{1,0:T(8,128)(2,1)} %bitcast.40), kind=kOutput, calls=%fused_computation.121 | convolution fusion | flops 2147483648 | bytes 8388608 | tf_op jit(solution)/shard_map/dot_general | solution.py:146
  265.2 1.2 fusion.36
  (83 shorter events, 8.4 us)
Async XLA Ops:
  0.0 51.2 %copy-start = (bf16[256,1024]{1,0:T(8,128)(2,1)S(1)}, bf16[256,1024]{1,0:T(8,128)(2,1)}, u32[]{:S(2)}) copy-start(bf16[256,1024]{1,0:T(8,128)(2,1)} %param.16) | copy-start | bytes 1572868
  5.1 20.9 %all-to-all-start = ((bf16[64,2,576]{2,1,0:T(2,128)(2,1)}), bf16[64,2,576]{2,1,0:T(2,128)(2,1)S(1)}, u32[]{:S(2)}, u32[]{:S(2)}) async-start(bf16[64,2,576]{2,1,0:T(2,128)(2,1)} %reshape.195), calls=%async_computation | async-start | bytes 327680 | tf_op jit(solution)/shard_map/all_to_all | solution.py:48
  26.7 10.1 %copy-start.6 = (bf16[2,256,1024]{2,1,0:T(8,128)(2,1)S(1)}, bf16[2,256,1024]{2,1,0:T(8,128)(2,1)}, u32[]{:S(2)}) copy-start(bf16[2,256,1024]{2,1,0:T(8,128)(2,1)} %param.17) | copy-start | bytes 3145732
  31.1 15.7 %all-to-all-start.1 = ((bf16[64,2,1536]{2,1,0:T(2,128)(2,1)}), bf16[64,2,1536]{2,1,0:T(2,128)(2,1)S(1)}, u32[]{:S(2)}, u32[]{:S(2)}) async-start(bf16[64,2,1536]{2,1,0:T(2,128)(2,1)} %reshape.197), calls=%async_computation.1 | async-start | bytes 786432 | tf_op jit(solution)/shard_map/all_to_all | solution.py:54
  50.0 1.2 copy-start.7
  51.8 1.0 copy-start.8
  52.8 9.0 %copy-start.9 = (s32[256,8]{0,1:T(8,128)S(1)}, s32[256,8]{0,1:T(8,128)}, u32[]{:S(2)}) copy-start(s32[256,8]{0,1:T(8,128)} %param.23) | copy-start | bytes 24580
  58.5 7.3 %collective-permute-start = (f32[256,2048]{1,0:T(8,128)}, f32[256,2048]{1,0:T(8,128)}, u32[]{:S(2)}, u32[]{:S(2)}) collective-permute-start(f32[256,2048]{1,0:T(8,128)} %convolution_bitcast_fusion), channel_id=1, source_target_pairs={{0,1},{1,0},{2,3},{3,2},{4,5},{5,4},{6,7},{7,6},{8,9},{9,8},{10,11... | collective-permute-start | bytes 6291464 | tf_op jit(solution)/shard_map/ppermute | solution.py:86
  62.1 6.7 %copy-start.10 = (f32[2048]{0:T(1024)S(1)}, f32[2048]{0:T(1024)}, u32[]{:S(2)}) copy-start(f32[2048]{0:T(1024)} %param.22) | copy-start | bytes 24580
  70.9 34.2 %all-to-all-start.2 = ((bf16[64,8,2048]{2,1,0:T(8,128)(2,1)}), bf16[64,8,2048]{2,1,0:T(8,128)(2,1)}, u32[]{:S(2)}, u32[]{:S(2)}) async-start(bf16[64,8,2048]{2,1,0:T(8,128)(2,1)} %fusion.1), calls=%async_computation.2 | async-start | bytes 4194304 | tf_op jit(solution)/shard_map/all_to_all | solution.py:114
  76.5 40.8 %collective-permute-start.1 = (bf16[2048,512]{1,0:T(8,128)(2,1)}, bf16[2048,512]{1,0:T(8,128)(2,1)}, u32[]{:S(2)}, u32[]{:S(2)}) collective-permute-start(bf16[2048,512]{1,0:T(8,128)(2,1)} %bitcast.195), channel_id=1, source_target_pairs={{0,1},{1,0},{2,3},{3,2},{4,5},{5,4},{6,7},{7,6},{8,9},{9,8},{10,11... | collective-permute-start | bytes 6291464 | tf_op jit(solution)/shard_map/ppermute | solution.py:39
  105.1 56.4 %all-to-all-start.4 = ((bf16[64,16,2048]{2,1,0:T(8,128)(2,1)}), bf16[64,16,2048]{2,1,0:T(8,128)(2,1)}, u32[]{:S(2)}, u32[]{:S(2)}) async-start(bf16[64,16,2048]{2,1,0:T(8,128)(2,1)} %bitcast.176), calls=%async_computation.4 | async-start | bytes 8388608 | tf_op jit(solution)/shard_map/all_to_all | solution.py:114
  111.5 11.2 %collective-permute-start.2 = (bf16[2048,512]{1,0:T(8,128)(2,1)}, bf16[2048,512]{1,0:T(8,128)(2,1)}, u32[]{:S(2)}, u32[]{:S(2)}) collective-permute-start(bf16[2048,512]{1,0:T(8,128)(2,1)} %bitcast.198), channel_id=1, source_target_pairs={{0,1},{1,0},{2,3},{3,2},{4,5},{5,4},{6,7},{7,6},{8,9},{9,8},{10,11... | collective-permute-start | bytes 6291464 | tf_op jit(solution)/shard_map/ppermute | solution.py:40
  117.3 5.4 %copy-start.12 = (bf16[1,2048,512]{2,1,0:T(8,128)(2,1)S(1)}, bf16[1,2048,512]{2,1,0:T(8,128)(2,1)}, u32[]{:S(2)}) copy-start(bf16[1,2048,512]{2,1,0:T(8,128)(2,1)} %param.26) | copy-start | bytes 6291460
  117.3 10.2 %collective-permute-start.3 = (bf16[512,2048]{0,1:T(8,128)(2,1)}, bf16[512,2048]{0,1:T(8,128)(2,1)S(1)}, u32[]{:S(2)}, u32[]{:S(2)}) collective-permute-start(bf16[512,2048]{0,1:T(8,128)(2,1)} %bitcast.180), channel_id=1, source_target_pairs={{0,1},{1,0},{2,3},{3,2},{4,5},{5,4},{6,7},{7,6},{8,9},{9,8},{10,11... | collective-permute-start | bytes 6291464 | tf_op jit(solution)/shard_map/ppermute | solution.py:41
  122.7 4.9 %copy-start.3 = (bf16[1,512,2048]{1,2,0:T(8,128)(2,1)S(1)}, bf16[1,512,2048]{1,2,0:T(8,128)(2,1)}, u32[]{:S(2)}) copy-start(bf16[1,512,2048]{1,2,0:T(8,128)(2,1)} %copy.101) | copy-start | bytes 6291460
  127.5 1.3 copy-start.14
  161.5 38.5 %all-to-all-start.3 = ((bf16[128,8,1024]{2,1,0:T(8,128)(2,1)}), bf16[128,8,1024]{2,1,0:T(8,128)(2,1)}, u32[]{:S(2)}, u32[]{:S(2)}) async-start(bf16[128,8,1024]{2,1,0:T(8,128)(2,1)} %bitcast.178), calls=%async_computation.3 | async-start | bytes 4194304 | tf_op jit(solution)/shard_map/all_to_all | solution.py:128
  171.9 7.7 %copy-start.13 = (bf16[1,2048,512]{2,1,0:T(8,128)(2,1)S(1)}, bf16[1,2048,512]{2,1,0:T(8,128)(2,1)}, u32[]{:S(2)}) copy-start(bf16[1,2048,512]{2,1,0:T(8,128)(2,1)} %param.26) | copy-start | bytes 6291460
  179.6 7.9 %copy-start.4 = (bf16[1,512,2048]{1,2,0:T(8,128)(2,1)S(1)}, bf16[1,512,2048]{1,2,0:T(8,128)(2,1)}, u32[]{:S(2)}) copy-start(bf16[1,512,2048]{1,2,0:T(8,128)(2,1)} %copy.101) | copy-start | bytes 6291460
  179.6 7.9 %copy-start.15 = (bf16[512,2048]{0,1:T(8,128)(2,1)S(1)}, bf16[512,2048]{0,1:T(8,128)(2,1)}, u32[]{:S(2)}) copy-start(bf16[512,2048]{0,1:T(8,128)(2,1)} %copy-done.14) | copy-start | bytes 6291460
  200.0 7.4 %copy-start.11 = (f32[256,8]{0,1:T(8,128)S(1)}, f32[256,8]{0,1:T(8,128)}, u32[]{:S(2)}) copy-start(f32[256,8]{0,1:T(8,128)} %param.24) | copy-start | bytes 24580
  200.0 59.8 %all-to-all-start.5 = ((bf16[128,16,1024]{2,1,0:T(8,128)(2,1)}), bf16[128,16,1024]{2,1,0:T(8,128)(2,1)}, u32[]{:S(2)}, u32[]{:S(2)}) async-start(bf16[128,16,1024]{2,1,0:T(8,128)(2,1)} %bitcast.177), calls=%async_computation.5 | async-start | bytes 8388608 | tf_op jit(solution)/shard_map/all_to_all | solution.py:128
  209.0 1.3 copy-start.5
  259.8 5.3 %copy-start.2 = (f32[512,1024]{1,0:T(8,128)S(1)}, f32[512,1024]{1,0:T(8,128)}, u32[]{:S(2)}) copy-start(f32[512,1024]{1,0:T(8,128)} %fusion.15) | copy-start | bytes 6291460
  259.8 6.6 %copy-start.1 = (bf16[256,1024]{1,0:T(8,128)(2,1)S(1)}, bf16[256,1024]{1,0:T(8,128)(2,1)}, u32[]{:S(2)}) copy-start(bf16[256,1024]{1,0:T(8,128)(2,1)} %param.16) | copy-start | bytes 1572868
